TPU v7x, 1024 devices: a whole 4x4x32 slice. The times are simulated.
1024 devices in a mesh: ctx: 16 (over z_hi, y), seq: 32 (over x, z_lo), head: 2 (over core).
Axes of the slice: x: 4, y: 4, z: 32 (z_hi: 4, z_lo: 8; z = z_hi * 8 + z_lo), core: 2. Of those that a mesh axis runs over, the one named last changes fastest.
Arguments:
- queries: bfloat16 [32, 2048, 4096], P('seq', 'ctx', 'head'), may hold values from -6 to 6
- keys_values: bfloat16 [32, 2048, 4, 256], P('seq', 'ctx', 'head'), may hold values from -6 to 6
- out_grad: bfloat16 [32, 2048, 4096], P('seq', 'ctx', 'head'), may hold values from -24 to 24
- doc_ids: int32 [32, 2048], P('seq'), may hold values from 0 to 15, never falling along the last dimension, each value on 1 to 256 neighbouring positions
- route: int32 [16, 32, 2], P('ctx'), may hold values from 0 to 31, as said below
Outputs:
- query_grad: bfloat16 [32, 2048, 4096], P('seq', 'ctx', 'head')
- kv_grad_owned: bfloat16 [32, 4096, 4, 256], P('seq', 'ctx', 'head')
Inputs may be any that keep to these rules, and one draw needn't show every extreme that they name: `doc_ids`: each document covers at most 256 consecutive positions, and one covers exactly that many. `route`: for each block index, the 2 pieces of one stretch go to distinct owners; an owner receives at most 4 pieces of one block index, and in every block index some owner receives exactly that many.
All inputs are finite; a program needn't handle non-finite values.
Results may differ from a plain program's by a relative error of at most 0.0057.
Values may be sent and summed in bfloat16 or wider, within the bound.
No kernel may reach another device: no remote copies, remote signals or barrier semaphores. Data moves between devices by JAX's collectives and lax.ppermute only.
A program may use at most 32 MiB of HBM per device.

v0:
```python
import jax
import jax.numpy as jnp
from jax import lax
from jax.sharding import PartitionSpec as P

HD = 128
PIECE = 64


def passed_along(shard, axis, by):
    peers = lax.axis_size(axis)
    pairs = [(i, i + by) for i in range(peers) if 0 <= i + by < peers]
    return lax.ppermute(shard, axis, pairs)


def from_behind(shard, axis, by):
    peers = lax.axis_size(axis)
    return lax.ppermute(shard, axis, [(i, (i + by) % peers) for i in range(peers)])


def shards(queries, keys_values, out_grad, doc_ids, route):
    tok_rows = queries.shape[1]
    kv_heads = keys_values.shape[2]
    group_size = queries.shape[2] // HD // kv_heads
    ctx_index = lax.axis_index("ctx")
    reach_steps = min(3, lax.axis_size("ctx"))
    scale_factor = HD ** (-0.5)
    query_four = queries[0].reshape(tok_rows, kv_heads, group_size, HD)
    grad_four = out_grad[0].reshape(tok_rows, kv_heads, group_size, HD)
    kv_local = keys_values[0]
    doc_row = doc_ids[0]
    offsets = jnp.arange(tok_rows, dtype=jnp.int32)
    query_pos = ctx_index * tok_rows + offsets
    query_doc = lax.dynamic_slice_in_dim(doc_row, ctx_index * tok_rows, tok_rows, 0)
    kv_blocks = [kv_local]
    current = kv_local
    for distance in range(1, reach_steps):
        current = passed_along(current, "ctx", 1)
        kv_blocks.append(current)
    totals = jnp.zeros((kv_heads, group_size, tok_rows), jnp.float32)
    out_acc = jnp.zeros((tok_rows, kv_heads, group_size, HD), jnp.float32)
    saved_exp = []
    for distance in range(reach_steps):
        scores = (
            jnp.einsum(
                "igad,jgd->gaij",
                query_four,
                kv_blocks[distance][..., :HD],
                preferred_element_type=jnp.float32,
            )
            * scale_factor
        )
        source = ctx_index - distance
        key_pos = source * tok_rows + offsets
        key_doc = lax.dynamic_slice_in_dim(doc_row, jnp.maximum(source, 0) * tok_rows, tok_rows, 0)
        exp_scores = jnp.where(
            (
                (query_doc[:, None] == key_doc[None, :])
                & (key_pos[None, :] <= query_pos[:, None])
                & (key_pos[None, :] >= 0)
            )[None, None],
            jnp.exp(scores),
            0.0,
        )
        saved_exp.append(exp_scores)
        totals = totals + jnp.sum(exp_scores, -1)
        out_acc = out_acc + jnp.einsum(
            "gaij,jgd->igad",
            exp_scores.astype(jnp.bfloat16),
            kv_blocks[distance][..., HD:],
            preferred_element_type=jnp.float32,
        )
    attended = out_acc / jnp.transpose(totals, (2, 0, 1))[..., None]
    delta = jnp.transpose(jnp.sum(grad_four.astype(jnp.float32) * attended, -1), (1, 2, 0))
    dq_acc = jnp.zeros((tok_rows, kv_heads, group_size, HD), jnp.float32)
    carried = None
    for distance in range(reach_steps):
        key_block = kv_blocks[distance][..., :HD]
        value_block = kv_blocks[distance][..., HD:]
        probs = saved_exp[distance] / totals[..., None]
        probs_low = probs.astype(jnp.bfloat16)
        grad_probs = jnp.einsum(
            "igad,jgd->gaij", grad_four, value_block, preferred_element_type=jnp.float32
        )
        score_low = (probs * (grad_probs - delta[..., None])).astype(jnp.bfloat16)
        dq_acc = dq_acc + jnp.einsum(
            "gaij,jgd->igad", score_low, key_block, preferred_element_type=jnp.float32
        )
        key_grad = (
            jnp.einsum("gaij,igad->jgd", score_low, query_four, preferred_element_type=jnp.float32)
            * scale_factor
        )
        value_grad = jnp.einsum(
            "gaij,igad->jgd", probs_low, grad_four, preferred_element_type=jnp.float32
        )
        term_kv = jnp.concatenate([key_grad, value_grad], -1)
        if distance == 0:
            carried = term_kv
        else:
            carried = from_behind(carried, "ctx", 1) + term_kv
    carried = from_behind(carried.astype(jnp.bfloat16), "ctx", 1 - reach_steps).astype(
        carried.dtype
    )
    query_grad = (
        (dq_acc * scale_factor)
        .astype(jnp.bfloat16)
        .reshape(1, tok_rows, kv_heads * group_size * HD)
    )
    kv_grad = carried.astype(jnp.bfloat16)
    seq_index = lax.axis_index("seq")
    seq_count = lax.axis_size("seq")
    piece_count = tok_rows // PIECE
    route_table = route[0]
    my_route = lax.dynamic_index_in_dim(route_table, seq_index, 0, keepdims=False)
    owner_ids = jnp.arange(seq_count, dtype=jnp.int32)
    select_out = (my_route[None, :] == owner_ids[:, None]).astype(jnp.bfloat16)
    piece_rows = kv_grad.reshape(piece_count, PIECE, kv_heads, 2 * HD)
    outgoing = jnp.einsum(
        "op,pxhw->oxhw", select_out, piece_rows, preferred_element_type=jnp.float32
    ).astype(jnp.bfloat16)
    incoming = lax.all_to_all(outgoing, "seq", split_axis=0, concat_axis=0, tiled=True)
    arrive_flag = jnp.sum((route_table == seq_index).astype(jnp.int32), 1)
    arrive_rank = jnp.cumsum(arrive_flag) - arrive_flag
    slot_ids = jnp.arange(2 * piece_count, dtype=jnp.int32)
    place_map = ((arrive_rank[None, :] == slot_ids[:, None]) & (arrive_flag[None, :] > 0)).astype(
        jnp.bfloat16
    )
    owned = jnp.einsum(
        "ks,sxhw->kxhw", place_map, incoming, preferred_element_type=jnp.float32
    ).astype(jnp.bfloat16)
    return (query_grad, owned.reshape(1, 2 * piece_count * PIECE, kv_heads, 2 * HD))


def solution(mesh):
    placed = (
        P("seq", "ctx", "head"),
        P("seq", "ctx", "head", None),
        P("seq", "ctx", "head"),
        P("seq", None),
        P("ctx", None, None),
    )
    return jax.shard_map(
        shards,
        mesh=mesh,
        in_specs=placed,
        out_specs=(P("seq", "ctx", "head"), P("seq", "ctx", "head", None)),
        check_vma=False,
    )
```

profile of v0, /device:TPU:24, one launch (start us, length us, event | category | flops | bytes accessed | tf_op | source)
XLA Modules:
  0.0 298.1 jit_solution(1689102294815897800)
XLA Ops:
  0.6 0.9 copy.164
  1.6 15.4 %collective-permute-start = (bf16[128,2,256]{2,0,1:T(8,128)(2,1)S(1)}, bf16[128,2,256]{2,0,1:T(8,128)(2,1)S(1)}, u32[]{:S(2)}, u32[]{:S(2)}) collective-permute-start(bf16[128,2,256]{2,0,1:T(8,128)(2,1)S(1)} %bitcast.203), channel_id=1, source_target_pairs={{0,64},{64,128},{128,192},{192,256},{256,320},{320,384},{384,448},... | collective-permute-start | bytes 393224 | tf_op jit(solution)/shard_map/ppermute | solution.py:13
  17.0 1.3 copy.156
  18.3 0.8 fusion.58
  19.1 0.8 and_and_fusion
  19.9 0.9 fusion.61
  21.2 1.0 copy.76
  22.2 13.2 %collective-permute-start.1 = (bf16[128,2,256]{2,0,1:T(8,128)(2,1)S(1)}, bf16[128,2,256]{2,0,1:T(8,128)(2,1)S(1)}, u32[]{:S(2)}, u32[]{:S(2)}) collective-permute-start(bf16[128,2,256]{2,0,1:T(8,128)(2,1)S(1)} %collective-permute-done), channel_id=1, source_target_pairs={{0,64},{64,128},{128,192},{192,256},{256,320},{320,384},{384,448},... | collective-permute-start | bytes 393224 | tf_op jit(solution)/shard_map/ppermute | solution.py:13
  35.5 1.1 fusion.62
  36.9 16.1 %collective-permute-done.1 = bf16[128,2,256]{2,0,1:T(8,128)(2,1)S(1)} collective-permute-done((bf16[128,2,256]{2,0,1:T(8,128)(2,1)S(1)}, bf16[128,2,256]{2,0,1:T(8,128)(2,1)S(1)}, u32[]{:S(2)}, u32[]{:S(2)}) %collective-permute-start.1) | collective-permute-done | bytes 131104 | tf_op jit(solution)/shard_map/ppermute | solution.py:13
  53.0 0.3 fusion.60
  53.7 0.4 fusion.25
  54.7 15.4 %collective-permute-start.2 = (f32[128,2,256]{0,2,1:T(8,128)S(1)}, f32[128,2,256]{0,2,1:T(8,128)S(1)}, u32[]{:S(2)}, u32[]{:S(2)}) collective-permute-start(f32[128,2,256]{0,2,1:T(8,128)S(1)} %pad_maximum_fusion), channel_id=1, source_target_pairs={{0,64},{64,128},{128,192},{192,256},{256,320},{320,384},{384,448},... | collective-permute-start | bytes 786440 | tf_op jit(solution)/shard_map/ppermute | solution.py:18
  71.4 12.3 %collective-permute-done.2 = f32[128,2,256]{0,2,1:T(8,128)S(1)} collective-permute-done((f32[128,2,256]{0,2,1:T(8,128)S(1)}, f32[128,2,256]{0,2,1:T(8,128)S(1)}, u32[]{:S(2)}, u32[]{:S(2)}) %collective-permute-start.2) | collective-permute-done | bytes 262176 | tf_op jit(solution)/shard_map/ppermute | solution.py:18
  83.7 15.6 %collective-permute-start.3 = (f32[128,2,256]{0,2,1:T(8,128)S(1)}, f32[128,2,256]{0,2,1:T(8,128)S(1)}, u32[]{:S(2)}, u32[]{:S(2)}) collective-permute-start(f32[128,2,256]{0,2,1:T(8,128)S(1)} %maximum_add_fusion), channel_id=1, source_target_pairs={{0,64},{64,128},{128,192},{192,256},{256,320},{320,384},{384,448},... | collective-permute-start | bytes 786440 | tf_op jit(solution)/shard_map/ppermute | solution.py:18
  100.0 17.7 %collective-permute-done.3 = f32[128,2,256]{0,2,1:T(8,128)S(1)} collective-permute-done((f32[128,2,256]{0,2,1:T(8,128)S(1)}, f32[128,2,256]{0,2,1:T(8,128)S(1)}, u32[]{:S(2)}, u32[]{:S(2)}) %collective-permute-start.3) | collective-permute-done | bytes 262176 | tf_op jit(solution)/shard_map/ppermute | solution.py:18
  117.7 1.9 collective-permute-start.4
  119.8 16.3 %collective-permute-done.4 = bf16[128,2,256]{0,2,1:T(8,128)(2,1)S(1)} collective-permute-done((bf16[128,2,256]{0,2,1:T(8,128)(2,1)S(1)}, bf16[128,2,256]{0,2,1:T(8,128)(2,1)S(1)}, u32[]{:S(2)}, u32[]{:S(2)}) %collective-permute-start.4) | collective-permute-done | bytes 131104 | tf_op jit(solution)/shard_map/ppermute | solution.py:18
  136.2 0.8 convolution_convert_fusion
  137.1 3.5 %copy.104 = bf16[32,64,2,256]{3,2,1,0:T(2,128)(2,1)} copy(bf16[32,64,2,256]{3,0,2,1:T(8,128)(2,1)S(1)} %convolution_convert_fusion) | data formatting | bytes 4194304 | tf_op jit(solution)/shard_map/convert_element_type | solution.py:120
  140.6 62.5 %all-to-all-start = ((bf16[32,64,2,256]{3,2,1,0:T(2,128)(2,1)}), bf16[32,64,2,256]{3,2,1,0:T(2,128)(2,1)S(1)}, u32[]{:S(2)}, u32[]{:S(2)}) async-start(bf16[32,64,2,256]{3,2,1,0:T(2,128)(2,1)} %copy.104), calls=%async_computation | async-start | bytes 4194304 | tf_op jit(solution)/shard_map/all_to_all | solution.py:121
  203.1 0.5 copy-done.5
  203.6 0.7 copy.92
  204.3 0.8 reduce-window.8
  205.1 0.6 reduce.1
  205.7 0.7 sub.39
  206.4 0.6 broadcast_compare_fusion
  207.3 1.4 convolution_add_fusion.1
  209.1 1.0 copy.107
  210.1 85.8 %all-to-all-done = bf16[32,64,2,256]{3,2,1,0:T(2,128)(2,1)S(1)} async-done(((bf16[32,64,2,256]{3,2,1,0:T(2,128)(2,1)}), bf16[32,64,2,256]{3,2,1,0:T(2,128)(2,1)S(1)}, u32[]{:S(2)}, u32[]{:S(2)}) %all-to-all-start) | async-done | bytes 2097184 | tf_op jit(solution)/shard_map/all_to_all | solution.py:121
  295.9 1.3 fusion.26
  297.2 1.0 copy.108
  (37 shorter events, 4.6 us)
Async XLA Ops:
  1.6 20.7 %collective-permute-start = (bf16[128,2,256]{2,0,1:T(8,128)(2,1)S(1)}, bf16[128,2,256]{2,0,1:T(8,128)(2,1)S(1)}, u32[]{:S(2)}, u32[]{:S(2)}) collective-permute-start(bf16[128,2,256]{2,0,1:T(8,128)(2,1)S(1)} %bitcast.203), channel_id=1, source_target_pairs={{0,64},{64,128},{128,192},{192,256},{256,320},{320,384},{384,448},... | collective-permute-start | bytes 393224 | tf_op jit(solution)/shard_map/ppermute | solution.py:13
  18.3 2.9 copy-start.1
  22.2 30.8 %collective-permute-start.1 = (bf16[128,2,256]{2,0,1:T(8,128)(2,1)S(1)}, bf16[128,2,256]{2,0,1:T(8,128)(2,1)S(1)}, u32[]{:S(2)}, u32[]{:S(2)}) collective-permute-start(bf16[128,2,256]{2,0,1:T(8,128)(2,1)S(1)} %collective-permute-done), channel_id=1, source_target_pairs={{0,64},{64,128},{128,192},{192,256},{256,320},{320,384},{384,448},... | collective-permute-start | bytes 393224 | tf_op jit(solution)/shard_map/ppermute | solution.py:13
  36.5 16.8 %copy-start.3 = (f32[2,8,128]{2,1,0:T(8,128)S(1)}, f32[2,8,128]{2,1,0:T(8,128)}, u32[]{:S(2)}) copy-start(f32[2,8,128]{2,1,0:T(8,128)} %get-tuple-element.17) | copy-start | bytes 24580
  36.5 16.8 %copy-start.2 = (bf16[1,128,2048]{1,2,0:T(8,128)(2,1)S(1)}, bf16[1,128,2048]{1,2,0:T(8,128)(2,1)}, u32[]{:S(2)}) copy-start(bf16[1,128,2048]{1,2,0:T(8,128)(2,1)} %copy.76) | copy-start | bytes 1572868
  54.7 28.9 %collective-permute-start.2 = (f32[128,2,256]{0,2,1:T(8,128)S(1)}, f32[128,2,256]{0,2,1:T(8,128)S(1)}, u32[]{:S(2)}, u32[]{:S(2)}) collective-permute-start(f32[128,2,256]{0,2,1:T(8,128)S(1)} %pad_maximum_fusion), channel_id=1, source_target_pairs={{0,64},{64,128},{128,192},{192,256},{256,320},{320,384},{384,448},... | collective-permute-start | bytes 786440 | tf_op jit(solution)/shard_map/ppermute | solution.py:18
  70.5 29.5 %copy-start = (bf16[2,8,128,128]{2,3,1,0:T(8,128)(2,1)}, bf16[2,8,128,128]{2,3,1,0:T(8,128)(2,1)S(1)}, u32[]{:S(2)}) copy-start(bf16[2,8,128,128]{2,3,1,0:T(8,128)(2,1)S(1)} %fusion.23) | copy-start | bytes 1572868
  83.7 33.9 %collective-permute-start.3 = (f32[128,2,256]{0,2,1:T(8,128)S(1)}, f32[128,2,256]{0,2,1:T(8,128)S(1)}, u32[]{:S(2)}, u32[]{:S(2)}) collective-permute-start(f32[128,2,256]{0,2,1:T(8,128)S(1)} %maximum_add_fusion), channel_id=1, source_target_pairs={{0,64},{64,128},{128,192},{192,256},{256,320},{320,384},{384,448},... | collective-permute-start | bytes 786440 | tf_op jit(solution)/shard_map/ppermute | solution.py:18
  99.7 20.0 %copy-start.4 = (s32[1,32,2]{1,2,0:T(2,128)S(1)}, s32[1,32,2]{1,2,0:T(2,128)}, u32[]{:S(2)}) copy-start(s32[1,32,2]{1,2,0:T(2,128)} %param.9) | copy-start | bytes 772
  117.7 18.4 %collective-permute-start.4 = (bf16[128,2,256]{0,2,1:T(8,128)(2,1)S(1)}, bf16[128,2,256]{0,2,1:T(8,128)(2,1)S(1)}, u32[]{:S(2)}, u32[]{:S(2)}) collective-permute-start(bf16[128,2,256]{0,2,1:T(8,128)(2,1)S(1)} %fusion.42), channel_id=1, source_target_pairs={{0,896},{64,960},{128,0},{192,64},{256,128},{320,192},{384,256},{4... | collective-permute-start | bytes 393224 | tf_op jit(solution)/shard_map/ppermute | solution.py:18
  140.6 155.3 %all-to-all-start = ((bf16[32,64,2,256]{3,2,1,0:T(2,128)(2,1)}), bf16[32,64,2,256]{3,2,1,0:T(2,128)(2,1)S(1)}, u32[]{:S(2)}, u32[]{:S(2)}) async-start(bf16[32,64,2,256]{3,2,1,0:T(2,128)(2,1)} %copy.104), calls=%async_computation | async-start | bytes 4194304 | tf_op jit(solution)/shard_map/all_to_all | solution.py:121
  203.1 0.5 copy-start.5
where the time goes:
time: 303 us; the launch traced here: 298 us
  waiting for transfers between devices  148 us (49%)
  starting transfers between devices  124 us (41%)
  local copies, waits for them, and re-layouts  11.1 us (4%)
  matrix products  10.3 us (3%)
  other arithmetic  3.62 us (1%)
    all_to_all x1, waiting for transfers between devices, shards(): lax.all_to_all(outgoing, 'seq', split_axis=0, concat_axis=0, tiled=True)  85.8 us
    all_to_all x1, starting transfers between devices, shards(): lax.all_to_all(outgoing, 'seq', split_axis=0, concat_axis=0, tiled=True)  62.5 us
    ppermute x3, waiting for transfers between devices, from_behind(): lax.ppermute(shard, axis, [(i, (i + by) % peers) for i in range(peers)])  46.2 us
    ppermute x3, starting transfers between devices, from_behind(): lax.ppermute(shard, axis, [(i, (i + by) % peers) for i in range(peers)])  33 us
    ppermute x2, starting transfers between devices, passed_along(): return lax.ppermute(shard, axis, pairs)  28.6 us
    ppermute x2, waiting for transfers between devices, passed_along(): return lax.ppermute(shard, axis, pairs)  16.1 us
  transfers between devices with their start and end apart: 6, of which 5 were waited for; matrix products, arithmetic and copies ran while one was open for 5% of the time, Pallas kernels for 0%

commit v1 on v0

--- a/solution.py
+++ b/solution.py
@@ -1,21 +1,16 @@
 import jax
 import jax.numpy as jnp
 from jax import lax
-from jax.sharding import PartitionSpec as P
+from jax.sharding import Mesh, PartitionSpec as P
 
 HD = 128
 PIECE = 64
 
 
-def passed_along(shard, axis, by):
+def shifted(shard, axis, by):
     peers = lax.axis_size(axis)
     pairs = [(i, i + by) for i in range(peers) if 0 <= i + by < peers]
     return lax.ppermute(shard, axis, pairs)
-
-
-def from_behind(shard, axis, by):
-    peers = lax.axis_size(axis)
-    return lax.ppermute(shard, axis, [(i, (i + by) % peers) for i in range(peers)])
 
 
 def shards(queries, keys_values, out_grad, doc_ids, route):
@@ -32,11 +27,7 @@
     offsets = jnp.arange(tok_rows, dtype=jnp.int32)
     query_pos = ctx_index * tok_rows + offsets
     query_doc = lax.dynamic_slice_in_dim(doc_row, ctx_index * tok_rows, tok_rows, 0)
-    kv_blocks = [kv_local]
-    current = kv_local
-    for distance in range(1, reach_steps):
-        current = passed_along(current, "ctx", 1)
-        kv_blocks.append(current)
+    kv_blocks = [kv_local] + [shifted(kv_local, "ctx", d) for d in range(1, reach_steps)]
     totals = jnp.zeros((kv_heads, group_size, tok_rows), jnp.float32)
     out_acc = jnp.zeros((tok_rows, kv_heads, group_size, HD), jnp.float32)
     saved_exp = []
@@ -73,7 +64,7 @@
     attended = out_acc / jnp.transpose(totals, (2, 0, 1))[..., None]
     delta = jnp.transpose(jnp.sum(grad_four.astype(jnp.float32) * attended, -1), (1, 2, 0))
     dq_acc = jnp.zeros((tok_rows, kv_heads, group_size, HD), jnp.float32)
-    carried = None
+    kv_sum = None
     for distance in range(reach_steps):
         key_block = kv_blocks[distance][..., :HD]
         value_block = kv_blocks[distance][..., HD:]
@@ -94,55 +85,72 @@
             "gaij,igad->jgd", probs_low, grad_four, preferred_element_type=jnp.float32
         )
         term_kv = jnp.concatenate([key_grad, value_grad], -1)
-        if distance == 0:
-            carried = term_kv
-        else:
-            carried = from_behind(carried, "ctx", 1) + term_kv
-    carried = from_behind(carried.astype(jnp.bfloat16), "ctx", 1 - reach_steps).astype(
-        carried.dtype
-    )
+        if distance > 0:
+            term_kv = shifted(term_kv, "ctx", -distance)
+        kv_sum = term_kv if kv_sum is None else kv_sum + term_kv
     query_grad = (
         (dq_acc * scale_factor)
         .astype(jnp.bfloat16)
         .reshape(1, tok_rows, kv_heads * group_size * HD)
     )
-    kv_grad = carried.astype(jnp.bfloat16)
-    seq_index = lax.axis_index("seq")
-    seq_count = lax.axis_size("seq")
+    kv_grad = kv_sum.astype(jnp.bfloat16)
+    inner = lax.axis_size("sz")
+    outer = lax.axis_size("sx")
+    row_index = lax.axis_index("sx")
+    col_index = lax.axis_index("sz")
     piece_count = tok_rows // PIECE
     route_table = route[0]
-    my_route = lax.dynamic_index_in_dim(route_table, seq_index, 0, keepdims=False)
-    owner_ids = jnp.arange(seq_count, dtype=jnp.int32)
-    select_out = (my_route[None, :] == owner_ids[:, None]).astype(jnp.bfloat16)
+    seq_count = route_table.shape[0]
     piece_rows = kv_grad.reshape(piece_count, PIECE, kv_heads, 2 * HD)
-    outgoing = jnp.einsum(
-        "op,pxhw->oxhw", select_out, piece_rows, preferred_element_type=jnp.float32
+    my_route = lax.dynamic_index_in_dim(route_table, row_index * inner + col_index, 0, keepdims=False)
+    col_ids = jnp.arange(inner, dtype=jnp.int32)
+    to_col = (my_route[None, :] % inner == col_ids[:, None]).astype(jnp.bfloat16)
+    first_out = jnp.einsum(
+        "cp,pxhw->cpxhw", to_col, piece_rows, preferred_element_type=jnp.bfloat16
+    )
+    first_in = lax.all_to_all(first_out, "sz", split_axis=0, concat_axis=0, tiled=True)
+    row_routes = lax.dynamic_slice_in_dim(route_table, row_index * inner, inner, 0)
+    owners = jnp.arange(seq_count, dtype=jnp.int32)
+    hits = (route_table[:, :, None] == owners[None, None, :]).astype(jnp.int32)
+    sends = jnp.sum(hits, 1)
+    ranks = jnp.cumsum(sends, 0) - sends
+    row_ranks = lax.dynamic_slice_in_dim(ranks, row_index * inner, inner, 0)
+    slot_ids = jnp.arange(2 * piece_count, dtype=jnp.int32)
+    target_rows = jnp.arange(outer, dtype=jnp.int32)
+    target_owner = target_rows * inner + col_index
+    piece_owner = row_routes
+    piece_rank = jnp.take_along_axis(row_ranks, piece_owner, axis=1)
+    second_map = (
+        (piece_owner[None, None, :, :] == target_owner[:, None, None, None])
+        & (piece_rank[None, None, :, :] == slot_ids[None, :, None, None])
     ).astype(jnp.bfloat16)
-    incoming = lax.all_to_all(outgoing, "seq", split_axis=0, concat_axis=0, tiled=True)
-    arrive_flag = jnp.sum((route_table == seq_index).astype(jnp.int32), 1)
-    arrive_rank = jnp.cumsum(arrive_flag) - arrive_flag
-    slot_ids = jnp.arange(2 * piece_count, dtype=jnp.int32)
-    place_map = ((arrive_rank[None, :] == slot_ids[:, None]) & (arrive_flag[None, :] > 0)).astype(
-        jnp.bfloat16
-    )
-    owned = jnp.einsum(
-        "ks,sxhw->kxhw", place_map, incoming, preferred_element_type=jnp.float32
+    second_out = jnp.einsum(
+        "tkzp,zpxhw->tkxhw", second_map, first_in, preferred_element_type=jnp.float32
     ).astype(jnp.bfloat16)
+    second_in = lax.all_to_all(second_out, "sx", split_axis=0, concat_axis=0, tiled=True)
+    owned = jnp.sum(second_in.astype(jnp.float32), 0).astype(jnp.bfloat16)
     return (query_grad, owned.reshape(1, 2 * piece_count * PIECE, kv_heads, 2 * HD))
 
 
 def solution(mesh):
+    seq_count = mesh.shape["seq"]
+    inner = 8 if seq_count % 8 == 0 else 1
+    split_mesh = Mesh(
+        mesh.devices.reshape(mesh.shape["ctx"], seq_count // inner, inner, mesh.shape["head"]),
+        ("ctx", "sx", "sz", "head"),
+    )
+    seq = ("sx", "sz")
     placed = (
-        P("seq", "ctx", "head"),
-        P("seq", "ctx", "head", None),
-        P("seq", "ctx", "head"),
-        P("seq", None),
+        P(seq, "ctx", "head"),
+        P(seq, "ctx", "head", None),
+        P(seq, "ctx", "head"),
+        P(seq, None),
         P("ctx", None, None),
     )
     return jax.shard_map(
         shards,
-        mesh=mesh,
+        mesh=split_mesh,
         in_specs=placed,
-        out_specs=(P("seq", "ctx", "head"), P("seq", "ctx", "head", None)),
+        out_specs=(P(seq, "ctx", "head"), P(seq, "ctx", "head", None)),
         check_vma=False,
     )

time: 303 us -> 230 us (0.76)
  the two profiles are of different devices: /device:TPU:24 before, /device:TPU:16 now
where the time goes in v1:
time: 230 us; the launch traced here: 229 us
  waiting for transfers between devices  119 us (52%)
  starting transfers between devices  85.2 us (37%)
  local copies, waits for them, and re-layouts  10.9 us (5%)
  matrix products  9.19 us (4%)
  other arithmetic  3.88 us (2%)
    ppermute x4, waiting for transfers between devices, shifted(): return lax.ppermute(shard, axis, pairs)  58.7 us
    all_to_all x1, starting transfers between devices, shards(): lax.all_to_all(first_out, 'sz', split_axis=0, concat_axis=0, tiled=True)  57.5 us
    all_to_all x1, waiting for transfers between devices, shards(): lax.all_to_all(first_out, 'sz', split_axis=0, concat_axis=0, tiled=True)  49.9 us
    ppermute x4, starting transfers between devices, shifted(): return lax.ppermute(shard, axis, pairs)  23.4 us
    all_to_all x1, waiting for transfers between devices, shards(): lax.all_to_all(second_out, 'sx', split_axis=0, concat_axis=0, tiled=True)  10.5 us
    unnamed x20, local copies, waits for them, and re-layouts  6.67 us
  transfers between devices with their start and end apart: 6, of which 4 were waited for; matrix products, arithmetic and copies ran while one was open for 5% of the time, Pallas kernels for 0%

profile of v1, /device:TPU:16, one launch (start us, length us, event | category | flops | bytes accessed | tf_op | source)
XLA Modules:
  0.0 229.2 jit_solution(17197260979012005314)
XLA Ops:
  0.6 0.9 copy.240
  1.6 15.5 %collective-permute-start.1 = (bf16[128,2,256]{2,0,1:T(8,128)(2,1)S(1)}, bf16[128,2,256]{2,0,1:T(8,128)(2,1)S(1)}, u32[]{:S(2)}, u32[]{:S(2)}) collective-permute-start(bf16[128,2,256]{2,0,1:T(8,128)(2,1)S(1)} %bitcast.215), channel_id=1, source_target_pairs={{0,128},{64,192},{128,256},{192,320},{256,384},{320,448},{384,512}... | collective-permute-start | bytes 393224 | tf_op jit(solution)/shard_map/ppermute | solution.py:13
  17.1 4.1 %collective-permute-start = (bf16[128,2,256]{2,0,1:T(8,128)(2,1)S(1)}, bf16[128,2,256]{2,0,1:T(8,128)(2,1)S(1)}, u32[]{:S(2)}, u32[]{:S(2)}) collective-permute-start(bf16[128,2,256]{2,0,1:T(8,128)(2,1)S(1)} %bitcast.216), channel_id=1, source_target_pairs={{0,64},{64,128},{128,192},{192,256},{256,320},{320,384},{384,448},... | collective-permute-start | bytes 393224 | tf_op jit(solution)/shard_map/ppermute | solution.py:13
  21.2 1.3 copy.234
  22.5 0.7 fusion.56
  23.3 0.8 and_and_fusion
  24.1 0.9 fusion.60
  25.4 0.7 copy-done.4
  26.1 1.0 copy.154
  27.1 0.9 fusion.48
  28.0 1.1 fusion.59
  29.1 0.4 fusion.61
  29.8 0.4 copy-done.5
  30.7 0.3 convolution_add_fusion.3
  31.1 0.4 fusion.23
  32.5 1.9 collective-permute-start.2
  35.0 1.9 collective-permute-start.3
  37.6 6.1 %collective-permute-done.2 = f32[128,2,256]{0,2,1:T(8,128)S(1)} collective-permute-done((f32[128,2,256]{0,2,1:T(8,128)S(1)}, f32[128,2,256]{0,2,1:T(8,128)S(1)}, u32[]{:S(2)}, u32[]{:S(2)}) %collective-permute-start.2) | collective-permute-done | bytes 262176 | tf_op jit(solution)/shard_map/ppermute | solution.py:13
  43.7 52.5 %collective-permute-done.3 = f32[128,2,256]{0,2,1:T(8,128)S(1)} collective-permute-done((f32[128,2,256]{0,2,1:T(8,128)S(1)}, f32[128,2,256]{0,2,1:T(8,128)S(1)}, u32[]{:S(2)}, u32[]{:S(2)}) %collective-permute-start.3) | collective-permute-done | bytes 262176 | tf_op jit(solution)/shard_map/ppermute | solution.py:13
  96.6 1.8 multiply_bitcast_fusion
  98.4 57.5 %all-to-all-start = ((bf16[8,2,64,2,256]{4,1,3,2,0:T(2,128)(2,1)}), bf16[8,2,64,2,256]{4,1,3,2,0:T(2,128)(2,1)S(1)}, u32[]{:S(2)}, u32[]{:S(2)}) async-start(bf16[8,2,64,2,256]{4,1,3,2,0:T(2,128)(2,1)} %multiply_bitcast_fusion), calls=%async_computation | async-start | bytes 2097152 | tf_op jit(solution)/shard_map/all_to_all | solution.py:111
  156.3 0.6 gather_fusion
  157.3 49.9 %all-to-all-done = bf16[8,2,64,2,256]{4,1,3,2,0:T(2,128)(2,1)S(1)} async-done(((bf16[8,2,64,2,256]{4,1,3,2,0:T(2,128)(2,1)}), bf16[8,2,64,2,256]{4,1,3,2,0:T(2,128)(2,1)S(1)}, u32[]{:S(2)}, u32[]{:S(2)}) %all-to-all-start) | async-done | bytes 1048608 | tf_op jit(solution)/shard_map/all_to_all | solution.py:111
  207.2 2.0 bitcast_convert_fusion
  209.2 4.3 %all-to-all-start.1 = ((bf16[4,4,64,2,256]{4,1,3,2,0:T(4,128)(2,1)}), bf16[4,4,64,2,256]{4,1,3,2,0:T(4,128)(2,1)S(1)}, u32[]{:S(2)}, u32[]{:S(2)}) async-start(bf16[4,4,64,2,256]{4,1,3,2,0:T(4,128)(2,1)} %bitcast_convert_fusion), calls=%async_computation.1 | async-start | bytes 2097152 | tf_op jit(solution)/shard_map/all_to_all | solution.py:130
  213.9 0.7 copy-done.1
  214.9 0.7 copy-done.3
  215.6 0.3 fusion.19
  216.0 1.0 copy.185
  217.0 10.5 %all-to-all-done.1 = bf16[4,4,64,2,256]{4,1,3,2,0:T(4,128)(2,1)S(1)} async-done(((bf16[4,4,64,2,256]{4,1,3,2,0:T(4,128)(2,1)}), bf16[4,4,64,2,256]{4,1,3,2,0:T(4,128)(2,1)S(1)}, u32[]{:S(2)}, u32[]{:S(2)}) %all-to-all-start.1) | async-done | bytes 1048608 | tf_op jit(solution)/shard_map/all_to_all | solution.py:130
  227.5 0.7 reduce_sum.62
  228.3 1.0 copy.186
  (51 shorter events, 5.2 us)
Async XLA Ops:
  1.6 26.4 %collective-permute-start.1 = (bf16[128,2,256]{2,0,1:T(8,128)(2,1)S(1)}, bf16[128,2,256]{2,0,1:T(8,128)(2,1)S(1)}, u32[]{:S(2)}, u32[]{:S(2)}) collective-permute-start(bf16[128,2,256]{2,0,1:T(8,128)(2,1)S(1)} %bitcast.215), channel_id=1, source_target_pairs={{0,128},{64,192},{128,256},{192,320},{256,384},{320,448},{384,512}... | collective-permute-start | bytes 393224 | tf_op jit(solution)/shard_map/ppermute | solution.py:13
  17.1 12.0 %collective-permute-start = (bf16[128,2,256]{2,0,1:T(8,128)(2,1)S(1)}, bf16[128,2,256]{2,0,1:T(8,128)(2,1)S(1)}, u32[]{:S(2)}, u32[]{:S(2)}) collective-permute-start(bf16[128,2,256]{2,0,1:T(8,128)(2,1)S(1)} %bitcast.216), channel_id=1, source_target_pairs={{0,64},{64,128},{128,192},{192,256},{256,320},{320,384},{384,448},... | collective-permute-start | bytes 393224 | tf_op jit(solution)/shard_map/ppermute | solution.py:13
  25.0 1.0 copy-start.4
  29.1 0.7 copy-start.6
  29.1 1.0 copy-start.5
  32.1 2.6 %copy-start = (bf16[2,8,128,128]{2,3,1,0:T(8,128)(2,1)}, bf16[2,8,128,128]{2,3,1,0:T(8,128)(2,1)S(1)}, u32[]{:S(2)}) copy-start(bf16[2,8,128,128]{2,3,1,0:T(8,128)(2,1)S(1)} %fusion.21) | copy-start | bytes 1572868
  32.5 11.3 %collective-permute-start.2 = (f32[128,2,256]{0,2,1:T(8,128)S(1)}, f32[128,2,256]{0,2,1:T(8,128)S(1)}, u32[]{:S(2)}, u32[]{:S(2)}) collective-permute-start(f32[128,2,256]{0,2,1:T(8,128)S(1)} %pad_maximum_fusion), channel_id=1, source_target_pairs={{64,0},{128,64},{192,128},{256,192},{320,256},{384,320},{448,384},... | collective-permute-start | bytes 786440 | tf_op jit(solution)/shard_map/ppermute | solution.py:13
  34.7 2.6 %copy-start.2 = (bf16[2,8,128,128]{2,3,1,0:T(8,128)(2,1)}, bf16[2,8,128,128]{2,3,1,0:T(8,128)(2,1)S(1)}, u32[]{:S(2)}) copy-start(bf16[2,8,128,128]{2,3,1,0:T(8,128)(2,1)S(1)} %fusion.20) | copy-start | bytes 1572868
  35.0 61.2 %collective-permute-start.3 = (f32[128,2,256]{0,2,1:T(8,128)S(1)}, f32[128,2,256]{0,2,1:T(8,128)S(1)}, u32[]{:S(2)}, u32[]{:S(2)}) collective-permute-start(f32[128,2,256]{0,2,1:T(8,128)S(1)} %pad_maximum_fusion.1), channel_id=1, source_target_pairs={{128,0},{192,64},{256,128},{320,192},{384,256},{448,320},{512,384}... | collective-permute-start | bytes 786440 | tf_op jit(solution)/shard_map/ppermute | solution.py:13
  98.4 57.5 %copy-start.7 = (s32[1,32,2]{1,2,0:T(2,128)S(1)}, s32[1,32,2]{1,2,0:T(2,128)}, u32[]{:S(2)}) copy-start(s32[1,32,2]{1,2,0:T(2,128)} %param.9) | copy-start | bytes 772
  98.4 108.8 %all-to-all-start = ((bf16[8,2,64,2,256]{4,1,3,2,0:T(2,128)(2,1)}), bf16[8,2,64,2,256]{4,1,3,2,0:T(2,128)(2,1)S(1)}, u32[]{:S(2)}, u32[]{:S(2)}) async-start(bf16[8,2,64,2,256]{4,1,3,2,0:T(2,128)(2,1)} %multiply_bitcast_fusion), calls=%async_computation | async-start | bytes 2097152 | tf_op jit(solution)/shard_map/all_to_all | solution.py:111
  209.2 18.3 %all-to-all-start.1 = ((bf16[4,4,64,2,256]{4,1,3,2,0:T(4,128)(2,1)}), bf16[4,4,64,2,256]{4,1,3,2,0:T(4,128)(2,1)S(1)}, u32[]{:S(2)}, u32[]{:S(2)}) async-start(bf16[4,4,64,2,256]{4,1,3,2,0:T(4,128)(2,1)} %bitcast_convert_fusion), calls=%async_computation.1 | async-start | bytes 2097152 | tf_op jit(solution)/shard_map/all_to_all | solution.py:130
  213.5 1.0 copy-start.1
  214.6 1.0 copy-start.3

commit v2 on v1

--- a/solution.py
+++ b/solution.py
@@ -86,7 +86,7 @@
         )
         term_kv = jnp.concatenate([key_grad, value_grad], -1)
         if distance > 0:
-            term_kv = shifted(term_kv, "ctx", -distance)
+            term_kv = shifted(term_kv.astype(jnp.bfloat16), "ctx", -distance).astype(jnp.float32)
         kv_sum = term_kv if kv_sum is None else kv_sum + term_kv
     query_grad = (
         (dq_acc * scale_factor)

time: 230 us -> 188 us (0.82)
  waiting for transfers between devices: 119 us -> 85.8 us
  starting transfers between devices: 85.2 us -> 77.4 us
    ppermute x4, waiting for transfers between devices: 58.7 us -> 28.1 us  [shifted(): return lax.ppermute(shard, axis, pairs)]
    all_to_all x1, starting transfers between devices: 57.5 us -> 49.6 us  [shards(): lax.all_to_all(first_out, 'sz', split_axis=0, concat_axis=0, tiled=True)]
    unnamed x20 -> x14, local copies, waits for them, and re-layouts: 6.67 us -> 5.27 us
  transfers between devices with their start and end apart: 6 -> 6, of which waited for: 4 -> 4; matrix products, arithmetic and copies ran while one was open for 5% -> 6% of each run, Pallas kernels for 0% -> 0%
where the time goes in v2:
time: 188 us; the launch traced here: 187 us
  waiting for transfers between devices  85.8 us (46%)
  starting transfers between devices  77.4 us (41%)
  local copies, waits for them, and re-layouts  9.47 us (5%)
  matrix products  9.26 us (5%)
  other arithmetic  4.46 us (2%)
    all_to_all x1, starting transfers between devices, shards(): lax.all_to_all(first_out, 'sz', split_axis=0, concat_axis=0, tiled=True)  49.6 us
    all_to_all x1, waiting for transfers between devices, shards(): lax.all_to_all(first_out, 'sz', split_axis=0, concat_axis=0, tiled=True)  48.9 us
    ppermute x4, waiting for transfers between devices, shifted(): return lax.ppermute(shard, axis, pairs)  28.1 us
    ppermute x4, starting transfers between devices, shifted(): return lax.ppermute(shard, axis, pairs)  23.4 us
    all_to_all x1, waiting for transfers between devices, shards(): lax.all_to_all(second_out, 'sx', split_axis=0, concat_axis=0, tiled=True)  8.83 us
    unnamed x14, local copies, waits for them, and re-layouts  5.27 us
    all_to_all x1, starting transfers between devices, shards(): lax.all_to_all(second_out, 'sx', split_axis=0, concat_axis=0, tiled=True)  4.3 us
  transfers between devices with their start and end apart: 6, of which 4 were waited for; matrix products, arithmetic and copies ran while one was open for 6% of the time, Pallas kernels for 0%

profile of v2, /device:TPU:16, one launch (start us, length us, event | category | flops | bytes accessed | tf_op | source)
XLA Modules:
  0.0 187.3 jit_solution(12392729277810119811)
XLA Ops:
  0.6 0.9 copy.240
  1.6 15.5 %collective-permute-start.1 = (bf16[128,2,256]{2,0,1:T(8,128)(2,1)S(1)}, bf16[128,2,256]{2,0,1:T(8,128)(2,1)S(1)}, u32[]{:S(2)}, u32[]{:S(2)}) collective-permute-start(bf16[128,2,256]{2,0,1:T(8,128)(2,1)S(1)} %bitcast.227), channel_id=1, source_target_pairs={{0,128},{64,192},{128,256},{192,320},{256,384},{320,448},{384,512}... | collective-permute-start | bytes 393224 | tf_op jit(solution)/shard_map/ppermute | solution.py:13
  17.1 4.1 %collective-permute-start = (bf16[128,2,256]{2,0,1:T(8,128)(2,1)S(1)}, bf16[128,2,256]{2,0,1:T(8,128)(2,1)S(1)}, u32[]{:S(2)}, u32[]{:S(2)}) collective-permute-start(bf16[128,2,256]{2,0,1:T(8,128)(2,1)S(1)} %bitcast.228), channel_id=1, source_target_pairs={{0,64},{64,128},{128,192},{192,256},{256,320},{320,384},{384,448},... | collective-permute-start | bytes 393224 | tf_op jit(solution)/shard_map/ppermute | solution.py:13
  21.2 1.3 copy.234
  22.5 0.7 fusion.62
  23.3 0.8 and_and_fusion
  24.1 0.9 fusion.66
  25.4 0.7 copy-done
  26.1 1.0 copy.154
  27.1 0.9 fusion.54
  28.0 0.6 fusion.53
  28.6 1.1 fusion.65
  29.7 0.4 fusion.67
  30.3 0.4 copy-done.1
  31.7 0.3 convolution_add_fusion.3
  32.0 0.4 fusion.23
  33.3 1.9 %collective-permute-start.2 = (bf16[128,2,256]{0,2,1:T(8,128)(2,1)S(1)}, bf16[128,2,256]{0,2,1:T(8,128)(2,1)S(1)}, u32[]{:S(2)}, u32[]{:S(2)}) collective-permute-start(bf16[128,2,256]{0,2,1:T(8,128)(2,1)S(1)} %pad_maximum_fusion), channel_id=1, source_target_pairs={{64,0},{128,64},{192,128},{256,192},{320,256},{384,320},{448,384},... | collective-permute-start | bytes 393224 | tf_op jit(solution)/shard_map/ppermute | solution.py:13
  35.9 1.9 %collective-permute-start.3 = (bf16[128,2,256]{0,2,1:T(8,128)(2,1)S(1)}, bf16[128,2,256]{0,2,1:T(8,128)(2,1)S(1)}, u32[]{:S(2)}, u32[]{:S(2)}) collective-permute-start(bf16[128,2,256]{0,2,1:T(8,128)(2,1)S(1)} %pad_maximum_fusion.1), channel_id=1, source_target_pairs={{128,0},{192,64},{256,128},{320,192},{384,256},{448,320},{512,384}... | collective-permute-start | bytes 393224 | tf_op jit(solution)/shard_map/ppermute | solution.py:13
  38.2 2.4 %collective-permute-done.2 = bf16[128,2,256]{0,2,1:T(8,128)(2,1)S(1)} collective-permute-done((bf16[128,2,256]{0,2,1:T(8,128)(2,1)S(1)}, bf16[128,2,256]{0,2,1:T(8,128)(2,1)S(1)}, u32[]{:S(2)}, u32[]{:S(2)}) %collective-permute-start.2) | collective-permute-done | bytes 131104 | tf_op jit(solution)/shard_map/ppermute | solution.py:13
  40.6 25.7 %collective-permute-done.3 = bf16[128,2,256]{0,2,1:T(8,128)(2,1)S(1)} collective-permute-done((bf16[128,2,256]{0,2,1:T(8,128)(2,1)S(1)}, bf16[128,2,256]{0,2,1:T(8,128)(2,1)S(1)}, u32[]{:S(2)}, u32[]{:S(2)}) %collective-permute-start.3) | collective-permute-done | bytes 131104 | tf_op jit(solution)/shard_map/ppermute | solution.py:13
  66.6 1.8 multiply_bitcast_fusion
  68.4 49.6 %all-to-all-start = ((bf16[8,2,64,2,256]{4,1,3,2,0:T(2,128)(2,1)}), bf16[8,2,64,2,256]{4,1,3,2,0:T(2,128)(2,1)S(1)}, u32[]{:S(2)}, u32[]{:S(2)}) async-start(bf16[8,2,64,2,256]{4,1,3,2,0:T(2,128)(2,1)} %multiply_bitcast_fusion), calls=%async_computation | async-start | bytes 2097152 | tf_op jit(solution)/shard_map/all_to_all | solution.py:111
  118.5 0.6 gather_fusion
  119.4 48.9 %all-to-all-done = bf16[8,2,64,2,256]{4,1,3,2,0:T(2,128)(2,1)S(1)} async-done(((bf16[8,2,64,2,256]{4,1,3,2,0:T(2,128)(2,1)}), bf16[8,2,64,2,256]{4,1,3,2,0:T(2,128)(2,1)S(1)}, u32[]{:S(2)}, u32[]{:S(2)}) %all-to-all-start) | async-done | bytes 1048608 | tf_op jit(solution)/shard_map/all_to_all | solution.py:111
  168.3 2.1 %bitcast_convert_fusion = bf16[4,4,64,2,256]{4,1,3,2,0:T(4,128)(2,1)} fusion(bf16[8,2,64,2,256]{4,1,3,2,0:T(2,128)(2,1)S(1)} %all-to-all-done, pred[4,8,2]{1,0,2:T(4,128)(4,1)S(1)} %iota_compare_fusion.2, pred[4,8,2]{1,2,0:T(4,128)(4,1)S(1)} %broadcast_compare_fusion), kind=kOutput, calls=%fused_computation.1 | convolution fusion | flops 17301760 | bytes 2097280 | tf_op jit(solution)/shard_map/tkzp,zpxhw->tkxhw/dot_general | solution.py:127
  170.4 4.3 %all-to-all-start.1 = ((bf16[4,4,64,2,256]{4,1,3,2,0:T(4,128)(2,1)}), bf16[4,4,64,2,256]{4,1,3,2,0:T(4,128)(2,1)S(1)}, u32[]{:S(2)}, u32[]{:S(2)}) async-start(bf16[4,4,64,2,256]{4,1,3,2,0:T(4,128)(2,1)} %bitcast_convert_fusion), calls=%async_computation.1 | async-start | bytes 2097152 | tf_op jit(solution)/shard_map/all_to_all | solution.py:130
  175.0 0.3 convolution_add_fusion.1
  175.4 0.4 fusion.19
  175.7 1.0 copy.185
  176.7 8.8 %all-to-all-done.1 = bf16[4,4,64,2,256]{4,1,3,2,0:T(4,128)(2,1)S(1)} async-done(((bf16[4,4,64,2,256]{4,1,3,2,0:T(4,128)(2,1)}), bf16[4,4,64,2,256]{4,1,3,2,0:T(4,128)(2,1)S(1)}, u32[]{:S(2)}, u32[]{:S(2)}) %all-to-all-start.1) | async-done | bytes 1048608 | tf_op jit(solution)/shard_map/all_to_all | solution.py:130
  185.6 0.7 reduce_sum.62
  186.3 1.0 copy.186
  (45 shorter events, 4.9 us)
Async XLA Ops:
  1.6 27.0 %collective-permute-start.1 = (bf16[128,2,256]{2,0,1:T(8,128)(2,1)S(1)}, bf16[128,2,256]{2,0,1:T(8,128)(2,1)S(1)}, u32[]{:S(2)}, u32[]{:S(2)}) collective-permute-start(bf16[128,2,256]{2,0,1:T(8,128)(2,1)S(1)} %bitcast.227), channel_id=1, source_target_pairs={{0,128},{64,192},{128,256},{192,320},{256,384},{320,448},{384,512}... | collective-permute-start | bytes 393224 | tf_op jit(solution)/shard_map/ppermute | solution.py:13
  17.1 12.6 %collective-permute-start = (bf16[128,2,256]{2,0,1:T(8,128)(2,1)S(1)}, bf16[128,2,256]{2,0,1:T(8,128)(2,1)S(1)}, u32[]{:S(2)}, u32[]{:S(2)}) collective-permute-start(bf16[128,2,256]{2,0,1:T(8,128)(2,1)S(1)} %bitcast.228), channel_id=1, source_target_pairs={{0,64},{64,128},{128,192},{192,256},{256,320},{320,384},{384,448},... | collective-permute-start | bytes 393224 | tf_op jit(solution)/shard_map/ppermute | solution.py:13
  25.1 1.0 copy-start
  29.6 0.7 copy-start.2
  29.7 1.0 copy-start.1
  33.3 7.3 %collective-permute-start.2 = (bf16[128,2,256]{0,2,1:T(8,128)(2,1)S(1)}, bf16[128,2,256]{0,2,1:T(8,128)(2,1)S(1)}, u32[]{:S(2)}, u32[]{:S(2)}) collective-permute-start(bf16[128,2,256]{0,2,1:T(8,128)(2,1)S(1)} %pad_maximum_fusion), channel_id=1, source_target_pairs={{64,0},{128,64},{192,128},{256,192},{320,256},{384,320},{448,384},... | collective-permute-start | bytes 393224 | tf_op jit(solution)/shard_map/ppermute | solution.py:13
  35.9 30.7 %copy-start.4 = (bf16[2,8]{0,1:T(8,128)(2,1)S(1)}, bf16[2,8]{0,1:T(8,128)(2,1)}, u32[]{:S(2)}) copy-start(bf16[2,8]{0,1:T(8,128)(2,1)} %fusion.53) | copy-start | bytes 100
  35.9 30.3 %collective-permute-start.3 = (bf16[128,2,256]{0,2,1:T(8,128)(2,1)S(1)}, bf16[128,2,256]{0,2,1:T(8,128)(2,1)S(1)}, u32[]{:S(2)}, u32[]{:S(2)}) collective-permute-start(bf16[128,2,256]{0,2,1:T(8,128)(2,1)S(1)} %pad_maximum_fusion.1), channel_id=1, source_target_pairs={{128,0},{192,64},{256,128},{320,192},{384,256},{448,320},{512,384}... | collective-permute-start | bytes 393224 | tf_op jit(solution)/shard_map/ppermute | solution.py:13
  68.4 49.6 %copy-start.3 = (s32[1,32,2]{1,2,0:T(2,128)S(1)}, s32[1,32,2]{1,2,0:T(2,128)}, u32[]{:S(2)}) copy-start(s32[1,32,2]{1,2,0:T(2,128)} %param.9) | copy-start | bytes 772
  68.4 99.9 %all-to-all-start = ((bf16[8,2,64,2,256]{4,1,3,2,0:T(2,128)(2,1)}), bf16[8,2,64,2,256]{4,1,3,2,0:T(2,128)(2,1)S(1)}, u32[]{:S(2)}, u32[]{:S(2)}) async-start(bf16[8,2,64,2,256]{4,1,3,2,0:T(2,128)(2,1)} %multiply_bitcast_fusion), calls=%async_computation | async-start | bytes 2097152 | tf_op jit(solution)/shard_map/all_to_all | solution.py:111
  170.4 15.2 %all-to-all-start.1 = ((bf16[4,4,64,2,256]{4,1,3,2,0:T(4,128)(2,1)}), bf16[4,4,64,2,256]{4,1,3,2,0:T(4,128)(2,1)S(1)}, u32[]{:S(2)}, u32[]{:S(2)}) async-start(bf16[4,4,64,2,256]{4,1,3,2,0:T(4,128)(2,1)} %bitcast_convert_fusion), calls=%async_computation.1 | async-start | bytes 2097152 | tf_op jit(solution)/shard_map/all_to_all | solution.py:130

commit v3 on v2

--- a/solution.py
+++ b/solution.py
@@ -1,3 +1,5 @@
+import functools
+
 import jax
 import jax.numpy as jnp
 from jax import lax
@@ -13,7 +15,13 @@
     return lax.ppermute(shard, axis, pairs)
 
 
-def shards(queries, keys_values, out_grad, doc_ids, route):
+def moved(shard, axis, pairs):
+    if not pairs:
+        return jnp.zeros_like(shard)
+    return lax.ppermute(shard, axis, pairs)
+
+
+def shards(near, queries, keys_values, out_grad, doc_ids, route):
     tok_rows = queries.shape[1]
     kv_heads = keys_values.shape[2]
     group_size = queries.shape[2] // HD // kv_heads
@@ -27,7 +35,14 @@
     offsets = jnp.arange(tok_rows, dtype=jnp.int32)
     query_pos = ctx_index * tok_rows + offsets
     query_doc = lax.dynamic_slice_in_dim(doc_row, ctx_index * tok_rows, tok_rows, 0)
-    kv_blocks = [kv_local] + [shifted(kv_local, "ctx", d) for d in range(1, reach_steps)]
+    blocks = lax.axis_size("ctx")
+    kv_blocks = [kv_local]
+    if reach_steps > 1:
+        kv_blocks.append(shifted(kv_local, "ctx", 1))
+    if reach_steps > 2:
+        relay = [(d - 1, d) for d in range(2, blocks) if near[d - 1][d] and not near[d - 2][d - 1]]
+        direct = [(d - 2, d) for d in range(2, blocks) if (d - 1, d) not in relay]
+        kv_blocks.append(moved(kv_local, "ctx", direct) + moved(kv_blocks[1], "ctx", relay))
     totals = jnp.zeros((kv_heads, group_size, tok_rows), jnp.float32)
     out_acc = jnp.zeros((tok_rows, kv_heads, group_size, HD), jnp.float32)
     saved_exp = []
@@ -64,7 +79,7 @@
     attended = out_acc / jnp.transpose(totals, (2, 0, 1))[..., None]
     delta = jnp.transpose(jnp.sum(grad_four.astype(jnp.float32) * attended, -1), (1, 2, 0))
     dq_acc = jnp.zeros((tok_rows, kv_heads, group_size, HD), jnp.float32)
-    kv_sum = None
+    terms = []
     for distance in range(reach_steps):
         key_block = kv_blocks[distance][..., :HD]
         value_block = kv_blocks[distance][..., HD:]
@@ -84,10 +99,20 @@
         value_grad = jnp.einsum(
             "gaij,igad->jgd", probs_low, grad_four, preferred_element_type=jnp.float32
         )
-        term_kv = jnp.concatenate([key_grad, value_grad], -1)
-        if distance > 0:
-            term_kv = shifted(term_kv.astype(jnp.bfloat16), "ctx", -distance).astype(jnp.float32)
-        kv_sum = term_kv if kv_sum is None else kv_sum + term_kv
+        terms.append(jnp.concatenate([key_grad, value_grad], -1))
+    kv_sum = terms[0]
+    if reach_steps == 2:
+        kv_sum = kv_sum + shifted(terms[1].astype(jnp.bfloat16), "ctx", -1).astype(jnp.float32)
+    elif reach_steps > 2:
+        ahead = [(b + 1, b + 2) for b in range(blocks - 2) if not near[b + 1][b] and near[b + 1][b + 2]]
+        back_one = [(b + 1, b) for b in range(blocks - 1) if (b + 1, b + 2) not in ahead]
+        back_two = [(b + 2, b) for b in range(blocks - 2)]
+        folded = terms[2] + moved(terms[1], "ctx", ahead)
+        kv_sum = (
+            kv_sum
+            + moved(terms[1].astype(jnp.bfloat16), "ctx", back_one).astype(jnp.float32)
+            + moved(folded.astype(jnp.bfloat16), "ctx", back_two).astype(jnp.float32)
+        )
     query_grad = (
         (dq_acc * scale_factor)
         .astype(jnp.bfloat16)
@@ -147,8 +172,11 @@
         P(seq, None),
         P("ctx", None, None),
     )
+    ctx_count = mesh.shape["ctx"]
+    heights = [mesh.devices[c, 0, 0].coords[2] for c in range(ctx_count)]
+    near = [[heights[a] == heights[b] for b in range(ctx_count)] for a in range(ctx_count)]
     return jax.shard_map(
-        shards,
+        functools.partial(shards, near),
         mesh=split_mesh,
         in_specs=placed,
         out_specs=(P(seq, "ctx", "head"), P(seq, "ctx", "head", None)),

time: 188 us -> 170 us (0.904)
  starting transfers between devices: 77.4 us -> 49.7 us
  waiting for transfers between devices: 85.8 us -> 93.4 us
    ppermute x0 -> x5, waiting for transfers between devices: none -> 32.7 us  [moved(): return lax.ppermute(shard, axis, pairs)]
    all_to_all x1, starting transfers between devices: 49.6 us -> 20.2 us  [shards(): lax.all_to_all(first_out, 'sz', split_axis=0, concat_axis=0, tiled=True)]
    ppermute x4 -> x1, waiting for transfers between devices: 28.1 us -> 0.01 us  [shifted(): return lax.ppermute(shard, axis, pairs)]
    ppermute x0 -> x5, starting transfers between devices: none -> 22 us  [moved(): return lax.ppermute(shard, axis, pairs)]
    ppermute x4 -> x1, starting transfers between devices: 23.4 us -> 3.19 us  [shifted(): return lax.ppermute(shard, axis, pairs)]
    unnamed x14 -> x22, local copies, waits for them, and re-layouts: 5.27 us -> 7.08 us
  transfers between devices with their start and end apart: 6 -> 8, of which waited for: 4 -> 4; matrix products, arithmetic and copies ran while one was open for 6% -> 7% of each run, Pallas kernels for 0% -> 0%
where the time goes in v3:
time: 170 us; the launch traced here: 169 us
  waiting for transfers between devices  93.4 us (55%)
  starting transfers between devices  49.7 us (29%)
  local copies, waits for them, and re-layouts  11.3 us (7%)
  matrix products  9.18 us (5%)
  other arithmetic  4.84 us (3%)
    all_to_all x1, waiting for transfers between devices, shards(): lax.all_to_all(first_out, 'sz', split_axis=0, concat_axis=0, tiled=True)  50 us
    ppermute x5, waiting for transfers between devices, moved(): return lax.ppermute(shard, axis, pairs)  32.7 us
    ppermute x5, starting transfers between devices, moved(): return lax.ppermute(shard, axis, pairs)  22 us
    all_to_all x1, starting transfers between devices, shards(): lax.all_to_all(first_out, 'sz', split_axis=0, concat_axis=0, tiled=True)  20.2 us
    all_to_all x1, waiting for transfers between devices, shards(): lax.all_to_all(second_out, 'sx', split_axis=0, concat_axis=0, tiled=True)  10.7 us
    unnamed x22, local copies, waits for them, and re-layouts  7.08 us
    all_to_all x1, starting transfers between devices, shards(): lax.all_to_all(second_out, 'sx', split_axis=0, concat_axis=0, tiled=True)  4.29 us
  transfers between devices with their start and end apart: 8, of which 4 were waited for; matrix products, arithmetic and copies ran while one was open for 7% of the time, Pallas kernels for 0%

profile of v3, /device:TPU:16, one launch (start us, length us, event | category | flops | bytes accessed | tf_op | source)
XLA Modules:
  0.0 169.4 jit_solution(13759205246242525890)
XLA Ops:
  0.6 0.9 copy.240
  1.6 3.2 %collective-permute-start = (bf16[128,2,256]{2,0,1:T(8,128)(2,1)S(1)}, bf16[128,2,256]{2,0,1:T(8,128)(2,1)S(1)}, u32[]{:S(2)}, u32[]{:S(2)}) collective-permute-start(bf16[128,2,256]{2,0,1:T(8,128)(2,1)S(1)} %bitcast.227), channel_id=1, source_target_pairs={{0,64},{64,128},{128,192},{192,256},{256,320},{320,384},{384,448},... | collective-permute-start | bytes 393224 | tf_op jit(solution)/shard_map/ppermute | solution.py:15
  4.8 15.8 %collective-permute-start.1 = (bf16[128,2,256]{2,0,1:T(8,128)(2,1)S(1)}, bf16[128,2,256]{2,0,1:T(8,128)(2,1)S(1)}, u32[]{:S(2)}, u32[]{:S(2)}) collective-permute-start(bf16[128,2,256]{2,0,1:T(8,128)(2,1)S(1)} %bitcast.228), channel_id=1, source_target_pairs={{0,128},{64,192},{128,256},{256,384},{320,448},{384,512},{512,640}... | collective-permute-start | bytes 393224 | tf_op jit(solution)/shard_map/ppermute | solution.py:21
  20.6 1.3 copy.234
  21.9 0.7 fusion.60
  22.7 0.8 and_and_fusion
  23.5 0.9 fusion.65
  24.8 0.7 copy-done.4
  25.5 1.0 copy.154
  26.5 0.9 fusion.52
  27.4 0.7 collective-permute-start.2
  28.1 1.1 fusion.66
  29.5 0.6 copy-done.6
  30.2 0.9 add.171
  31.8 0.4 fusion.26
  32.9 0.4 copy-done
  34.3 3.0 %collective-permute-start.3 = (bf16[128,2,256]{0,2,1:T(8,128)(2,1)S(1)}, bf16[128,2,256]{0,2,1:T(8,128)(2,1)S(1)}, u32[]{:S(2)}, u32[]{:S(2)}) collective-permute-start(bf16[128,2,256]{0,2,1:T(8,128)(2,1)S(1)} %fusion.62), channel_id=1, source_target_pairs={{64,0},{128,64},{192,128},{320,256},{384,320},{448,384},{576,512},... | collective-permute-start | bytes 393224 | tf_op jit(solution)/shard_map/ppermute | solution.py:21
  37.2 0.7 collective-permute-start.4
  38.6 1.9 %collective-permute-start.5 = (bf16[128,2,256]{0,2,1:T(8,128)(2,1)S(1)}, bf16[128,2,256]{0,2,1:T(8,128)(2,1)S(1)}, u32[]{:S(2)}, u32[]{:S(2)}) collective-permute-start(bf16[128,2,256]{0,2,1:T(8,128)(2,1)S(1)} %fusion.44), channel_id=1, source_target_pairs={{128,0},{192,64},{256,128},{320,192},{384,256},{448,320},{512,384}... | collective-permute-start | bytes 393224 | tf_op jit(solution)/shard_map/ppermute | solution.py:21
  41.1 32.4 %collective-permute-done.5 = bf16[128,2,256]{0,2,1:T(8,128)(2,1)S(1)} collective-permute-done((bf16[128,2,256]{0,2,1:T(8,128)(2,1)S(1)}, bf16[128,2,256]{0,2,1:T(8,128)(2,1)S(1)}, u32[]{:S(2)}, u32[]{:S(2)}) %collective-permute-start.5) | collective-permute-done | bytes 131104 | tf_op jit(solution)/shard_map/ppermute | solution.py:21
  73.8 1.8 %multiply_bitcast_fusion = bf16[8,2,64,2,256]{4,1,3,2,0:T(2,128)(2,1)} fusion(bf16[2,8]{0,1:T(8,128)(2,1)S(1)} %fusion.51, bf16[2,64,2,256]{3,0,2,1:T(2,128)(2,1)S(1)} %copy.182), kind=kLoop, calls=%fused_computation.53 | loop fusion | flops 524288 | bytes 1179680 | tf_op jit(solution)/shard_map/cp,pxhw->cpxhw/transpose | solution.py:133
  75.7 20.2 %all-to-all-start = ((bf16[8,2,64,2,256]{4,1,3,2,0:T(2,128)(2,1)}), bf16[8,2,64,2,256]{4,1,3,2,0:T(2,128)(2,1)S(1)}, u32[]{:S(2)}, u32[]{:S(2)}) async-start(bf16[8,2,64,2,256]{4,1,3,2,0:T(2,128)(2,1)} %multiply_bitcast_fusion), calls=%async_computation | async-start | bytes 2097152 | tf_op jit(solution)/shard_map/all_to_all | solution.py:136
  96.3 0.6 gather_fusion
  97.3 50.0 %all-to-all-done = bf16[8,2,64,2,256]{4,1,3,2,0:T(2,128)(2,1)S(1)} async-done(((bf16[8,2,64,2,256]{4,1,3,2,0:T(2,128)(2,1)}), bf16[8,2,64,2,256]{4,1,3,2,0:T(2,128)(2,1)S(1)}, u32[]{:S(2)}, u32[]{:S(2)}) %all-to-all-start) | async-done | bytes 1048608 | tf_op jit(solution)/shard_map/all_to_all | solution.py:136
  147.3 2.0 %bitcast_convert_fusion = bf16[4,4,64,2,256]{4,1,3,2,0:T(4,128)(2,1)} fusion(bf16[8,2,64,2,256]{4,1,3,2,0:T(2,128)(2,1)S(1)} %all-to-all-done, pred[4,8,2]{1,0,2:T(4,128)(4,1)S(1)} %iota_compare_fusion.2, pred[4,8,2]{1,2,0:T(4,128)(4,1)S(1)} %broadcast_compare_fusion), kind=kOutput, calls=%fused_computation.1 | convolution fusion | flops 17301760 | bytes 2097280 | tf_op jit(solution)/shard_map/tkzp,zpxhw->tkxhw/dot_general | solution.py:152
  149.3 4.3 %all-to-all-start.1 = ((bf16[4,4,64,2,256]{4,1,3,2,0:T(4,128)(2,1)}), bf16[4,4,64,2,256]{4,1,3,2,0:T(4,128)(2,1)S(1)}, u32[]{:S(2)}, u32[]{:S(2)}) async-start(bf16[4,4,64,2,256]{4,1,3,2,0:T(4,128)(2,1)} %bitcast_convert_fusion), calls=%async_computation.1 | async-start | bytes 2097152 | tf_op jit(solution)/shard_map/all_to_all | solution.py:155
  153.9 0.7 copy-done.1
  155.0 0.7 copy-done.3
  156.0 1.0 copy.185
  157.0 10.7 %all-to-all-done.1 = bf16[4,4,64,2,256]{4,1,3,2,0:T(4,128)(2,1)S(1)} async-done(((bf16[4,4,64,2,256]{4,1,3,2,0:T(4,128)(2,1)}), bf16[4,4,64,2,256]{4,1,3,2,0:T(4,128)(2,1)S(1)}, u32[]{:S(2)}, u32[]{:S(2)}) %all-to-all-start.1) | async-done | bytes 1048608 | tf_op jit(solution)/shard_map/all_to_all | solution.py:155
  167.7 0.7 reduce_sum.62
  168.5 1.0 copy.186
  (59 shorter events, 6.3 us)
Async XLA Ops:
  1.6 25.8 %collective-permute-start = (bf16[128,2,256]{2,0,1:T(8,128)(2,1)S(1)}, bf16[128,2,256]{2,0,1:T(8,128)(2,1)S(1)}, u32[]{:S(2)}, u32[]{:S(2)}) collective-permute-start(bf16[128,2,256]{2,0,1:T(8,128)(2,1)S(1)} %bitcast.227), channel_id=1, source_target_pairs={{0,64},{64,128},{128,192},{192,256},{256,320},{320,384},{384,448},... | collective-permute-start | bytes 393224 | tf_op jit(solution)/shard_map/ppermute | solution.py:15
  4.8 24.8 %collective-permute-start.1 = (bf16[128,2,256]{2,0,1:T(8,128)(2,1)S(1)}, bf16[128,2,256]{2,0,1:T(8,128)(2,1)S(1)}, u32[]{:S(2)}, u32[]{:S(2)}) collective-permute-start(bf16[128,2,256]{2,0,1:T(8,128)(2,1)S(1)} %bitcast.228), channel_id=1, source_target_pairs={{0,128},{64,192},{128,256},{256,384},{320,448},{384,512},{512,640}... | collective-permute-start | bytes 393224 | tf_op jit(solution)/shard_map/ppermute | solution.py:21
  24.4 1.0 copy-start.4
  27.4 2.8 %collective-permute-start.2 = (bf16[128,2,256]{2,0,1:T(8,128)(2,1)S(1)}, bf16[128,2,256]{2,0,1:T(8,128)(2,1)S(1)}, u32[]{:S(2)}, u32[]{:S(2)}) collective-permute-start(bf16[128,2,256]{2,0,1:T(8,128)(2,1)S(1)} %collective-permute-done), channel_id=1, source_target_pairs={{256,320},{512,576},{768,832},{257,321},{513,577},{769,833},{258,3... | collective-permute-start | bytes 393224 | tf_op jit(solution)/shard_map/ppermute | solution.py:21
  29.5 2.0 %copy-start.7 = (f32[2,8,128]{2,1,0:T(8,128)S(1)}, f32[2,8,128]{2,1,0:T(8,128)}, u32[]{:S(2)}) copy-start(f32[2,8,128]{2,1,0:T(8,128)} %get-tuple-element.23) | copy-start | bytes 24580
  29.5 2.0 %copy-start.5 = (bf16[1,128,2048]{1,2,0:T(8,128)(2,1)S(1)}, bf16[1,128,2048]{1,2,0:T(8,128)(2,1)}, u32[]{:S(2)}) copy-start(bf16[1,128,2048]{1,2,0:T(8,128)(2,1)} %copy.154) | copy-start | bytes 1572868
  29.5 0.7 copy-start.6
  32.5 0.8 copy-start
  33.6 4.3 %copy-start.2 = (bf16[2,8,128,128]{2,3,1,0:T(8,128)(2,1)}, bf16[2,8,128,128]{2,3,1,0:T(8,128)(2,1)S(1)}, u32[]{:S(2)}) copy-start(bf16[2,8,128,128]{2,3,1,0:T(8,128)(2,1)S(1)} %fusion.23) | copy-start | bytes 1572868
  34.3 6.9 %collective-permute-start.3 = (bf16[128,2,256]{0,2,1:T(8,128)(2,1)S(1)}, bf16[128,2,256]{0,2,1:T(8,128)(2,1)S(1)}, u32[]{:S(2)}, u32[]{:S(2)}) collective-permute-start(bf16[128,2,256]{0,2,1:T(8,128)(2,1)S(1)} %fusion.62), channel_id=1, source_target_pairs={{64,0},{128,64},{192,128},{320,256},{384,320},{448,384},{576,512},... | collective-permute-start | bytes 393224 | tf_op jit(solution)/shard_map/ppermute | solution.py:21
  37.2 1.3 collective-permute-start.4
  38.6 34.9 %collective-permute-start.5 = (bf16[128,2,256]{0,2,1:T(8,128)(2,1)S(1)}, bf16[128,2,256]{0,2,1:T(8,128)(2,1)S(1)}, u32[]{:S(2)}, u32[]{:S(2)}) collective-permute-start(bf16[128,2,256]{0,2,1:T(8,128)(2,1)S(1)} %fusion.44), channel_id=1, source_target_pairs={{128,0},{192,64},{256,128},{320,192},{384,256},{448,320},{512,384}... | collective-permute-start | bytes 393224 | tf_op jit(solution)/shard_map/ppermute | solution.py:21
  75.7 20.2 %copy-start.8 = (s32[1,32,2]{1,2,0:T(2,128)S(1)}, s32[1,32,2]{1,2,0:T(2,128)}, u32[]{:S(2)}) copy-start(s32[1,32,2]{1,2,0:T(2,128)} %param.9) | copy-start | bytes 772
  75.7 71.6 %all-to-all-start = ((bf16[8,2,64,2,256]{4,1,3,2,0:T(2,128)(2,1)}), bf16[8,2,64,2,256]{4,1,3,2,0:T(2,128)(2,1)S(1)}, u32[]{:S(2)}, u32[]{:S(2)}) async-start(bf16[8,2,64,2,256]{4,1,3,2,0:T(2,128)(2,1)} %multiply_bitcast_fusion), calls=%async_computation | async-start | bytes 2097152 | tf_op jit(solution)/shard_map/all_to_all | solution.py:136
  149.3 18.4 %all-to-all-start.1 = ((bf16[4,4,64,2,256]{4,1,3,2,0:T(4,128)(2,1)}), bf16[4,4,64,2,256]{4,1,3,2,0:T(4,128)(2,1)S(1)}, u32[]{:S(2)}, u32[]{:S(2)}) async-start(bf16[4,4,64,2,256]{4,1,3,2,0:T(4,128)(2,1)} %bitcast_convert_fusion), calls=%async_computation.1 | async-start | bytes 2097152 | tf_op jit(solution)/shard_map/all_to_all | solution.py:155
  153.6 1.0 copy-start.1
  154.6 1.0 copy-start.3

commit v4 on v3

--- a/solution.py
+++ b/solution.py
@@ -21,7 +21,7 @@
     return lax.ppermute(shard, axis, pairs)
 
 
-def shards(near, queries, keys_values, out_grad, doc_ids, route):
+def shards(near, column_mate, queries, keys_values, out_grad, doc_ids, route):
     tok_rows = queries.shape[1]
     kv_heads = keys_values.shape[2]
     group_size = queries.shape[2] // HD // kv_heads
@@ -41,8 +41,17 @@
         kv_blocks.append(shifted(kv_local, "ctx", 1))
     if reach_steps > 2:
         relay = [(d - 1, d) for d in range(2, blocks) if near[d - 1][d] and not near[d - 2][d - 1]]
-        direct = [(d - 2, d) for d in range(2, blocks) if (d - 1, d) not in relay]
-        kv_blocks.append(moved(kv_local, "ctx", direct) + moved(kv_blocks[1], "ctx", relay))
+        over = [(d - 2, m) for d in range(2, blocks) for m in [column_mate[d - 2][d]]
+                if (d - 1, d) not in relay and not near[d - 2][d] and m is not None]
+        down = [(m, d) for d in range(2, blocks) for m in [column_mate[d - 2][d]]
+                if (d - 1, d) not in relay and not near[d - 2][d] and m is not None]
+        direct = [(d - 2, d) for d in range(2, blocks) if (d - 1, d) not in relay and (d - 2, d) not in
+                  [(a, b) for (a, _), (_, b) in zip(over, down)]]
+        kv_blocks.append(
+            moved(kv_local, "ctx", direct)
+            + moved(kv_blocks[1], "ctx", relay)
+            + moved(moved(kv_local, "ctx", over), "ctx", down)
+        )
     totals = jnp.zeros((kv_heads, group_size, tok_rows), jnp.float32)
     out_acc = jnp.zeros((tok_rows, kv_heads, group_size, HD), jnp.float32)
     saved_exp = []
@@ -175,8 +184,17 @@
     ctx_count = mesh.shape["ctx"]
     heights = [mesh.devices[c, 0, 0].coords[2] for c in range(ctx_count)]
     near = [[heights[a] == heights[b] for b in range(ctx_count)] for a in range(ctx_count)]
+    places = [tuple(mesh.devices[c, 0, 0].coords) for c in range(ctx_count)]
+    column_mate = [
+        [
+            next((m for m in range(ctx_count) if m != b and places[m][1] == places[a][1]
+                  and places[m][2] == places[b][2]), None)
+            for b in range(ctx_count)
+        ]
+        for a in range(ctx_count)
+    ]
     return jax.shard_map(
-        functools.partial(shards, near),
+        functools.partial(shards, near, column_mate),
         mesh=split_mesh,
         in_specs=placed,
         out_specs=(P(seq, "ctx", "head"), P(seq, "ctx", "head", None)),

time: 170 us -> 175 us (1.029)
  the two profiles are of different devices: /device:TPU:16 before, /device:TPU:24 now
where the time goes in v4:
time: 175 us; the launch traced here: 174 us
  waiting for transfers between devices  98.5 us (56%)
  starting transfers between devices  49.5 us (28%)
  local copies, waits for them, and re-layouts  11.3 us (6%)
  matrix products  9.19 us (5%)
  other arithmetic  4.84 us (3%)
    all_to_all x1, waiting for transfers between devices, shards(): lax.all_to_all(first_out, 'sz', split_axis=0, concat_axis=0, tiled=True)  49.8 us
    ppermute x7, waiting for transfers between devices, moved(): return lax.ppermute(shard, axis, pairs)  38.6 us
    ppermute x7, starting transfers between devices, moved(): return lax.ppermute(shard, axis, pairs)  16.9 us
    ppermute x1, starting transfers between devices, shifted(): return lax.ppermute(shard, axis, pairs)  15.4 us
    all_to_all x1, starting transfers between devices, shards(): lax.all_to_all(first_out, 'sz', split_axis=0, concat_axis=0, tiled=True)  13 us
    all_to_all x1, waiting for transfers between devices, shards(): lax.all_to_all(second_out, 'sx', split_axis=0, concat_axis=0, tiled=True)  10.1 us
    unnamed x22, local copies, waits for them, and re-layouts  7.07 us
    all_to_all x1, starting transfers between devices, shards(): lax.all_to_all(second_out, 'sx', split_axis=0, concat_axis=0, tiled=True)  4.28 us
  transfers between devices with their start and end apart: 10, of which 3 were waited for; matrix products, arithmetic and copies ran while one was open for 7% of the time, Pallas kernels for 0%

profile of v4, /device:TPU:24, one launch (start us, length us, event | category | flops | bytes accessed | tf_op | source)
XLA Modules:
  0.0 174.4 jit_solution(3825052669011149423)
XLA Ops:
  0.6 0.9 copy.240
  1.6 15.4 %collective-permute-start = (bf16[128,2,256]{2,0,1:T(8,128)(2,1)S(1)}, bf16[128,2,256]{2,0,1:T(8,128)(2,1)S(1)}, u32[]{:S(2)}, u32[]{:S(2)}) collective-permute-start(bf16[128,2,256]{2,0,1:T(8,128)(2,1)S(1)} %bitcast.227), channel_id=1, source_target_pairs={{0,64},{64,128},{128,192},{192,256},{256,320},{320,384},{384,448},... | collective-permute-start | bytes 393224 | tf_op jit(solution)/shard_map/ppermute | solution.py:15
  16.9 1.3 collective-permute-start.3
  18.3 1.3 collective-permute-start.1
  19.6 1.3 copy.234
  20.9 0.7 fusion.60
  21.7 0.8 and_and_fusion
  22.5 0.9 fusion.65
  23.8 0.7 copy-done.4
  24.5 1.0 copy.154
  25.5 0.9 fusion.52
  26.4 0.7 collective-permute-start.2
  27.1 0.7 collective-permute-start.4
  27.7 1.1 fusion.66
  29.2 0.6 copy-done.6
  29.9 0.9 add_add_fusion
  33.9 5.5 %collective-permute-start.5 = (bf16[128,2,256]{0,2,1:T(8,128)(2,1)S(1)}, bf16[128,2,256]{0,2,1:T(8,128)(2,1)S(1)}, u32[]{:S(2)}, u32[]{:S(2)}) collective-permute-start(bf16[128,2,256]{0,2,1:T(8,128)(2,1)S(1)} %fusion.62), channel_id=1, source_target_pairs={{64,0},{128,64},{192,128},{320,256},{384,320},{448,384},{576,512},... | collective-permute-start | bytes 393224 | tf_op jit(solution)/shard_map/ppermute | solution.py:21
  39.5 0.7 collective-permute-start.6
  40.8 6.7 %collective-permute-start.7 = (bf16[128,2,256]{0,2,1:T(8,128)(2,1)S(1)}, bf16[128,2,256]{0,2,1:T(8,128)(2,1)S(1)}, u32[]{:S(2)}, u32[]{:S(2)}) collective-permute-start(bf16[128,2,256]{0,2,1:T(8,128)(2,1)S(1)} %fusion.44), channel_id=1, source_target_pairs={{128,0},{192,64},{256,128},{320,192},{384,256},{448,320},{512,384}... | collective-permute-start | bytes 393224 | tf_op jit(solution)/shard_map/ppermute | solution.py:21
  47.9 38.6 %collective-permute-done.7 = bf16[128,2,256]{0,2,1:T(8,128)(2,1)S(1)} collective-permute-done((bf16[128,2,256]{0,2,1:T(8,128)(2,1)S(1)}, bf16[128,2,256]{0,2,1:T(8,128)(2,1)S(1)}, u32[]{:S(2)}, u32[]{:S(2)}) %collective-permute-start.7) | collective-permute-done | bytes 131104 | tf_op jit(solution)/shard_map/ppermute | solution.py:21
  86.8 1.8 %multiply_bitcast_fusion = bf16[8,2,64,2,256]{4,1,3,2,0:T(2,128)(2,1)} fusion(bf16[2,8]{0,1:T(8,128)(2,1)S(1)} %fusion.51, bf16[2,64,2,256]{3,0,2,1:T(2,128)(2,1)S(1)} %copy.182), kind=kLoop, calls=%fused_computation.53 | loop fusion | flops 524288 | bytes 1179680 | tf_op jit(solution)/shard_map/cp,pxhw->cpxhw/transpose | solution.py:142
  88.6 13.0 %all-to-all-start = ((bf16[8,2,64,2,256]{4,1,3,2,0:T(2,128)(2,1)}), bf16[8,2,64,2,256]{4,1,3,2,0:T(2,128)(2,1)S(1)}, u32[]{:S(2)}, u32[]{:S(2)}) async-start(bf16[8,2,64,2,256]{4,1,3,2,0:T(2,128)(2,1)} %multiply_bitcast_fusion), calls=%async_computation | async-start | bytes 2097152 | tf_op jit(solution)/shard_map/all_to_all | solution.py:145
  102.1 0.6 gather_fusion
  103.0 49.8 %all-to-all-done = bf16[8,2,64,2,256]{4,1,3,2,0:T(2,128)(2,1)S(1)} async-done(((bf16[8,2,64,2,256]{4,1,3,2,0:T(2,128)(2,1)}), bf16[8,2,64,2,256]{4,1,3,2,0:T(2,128)(2,1)S(1)}, u32[]{:S(2)}, u32[]{:S(2)}) %all-to-all-start) | async-done | bytes 1048608 | tf_op jit(solution)/shard_map/all_to_all | solution.py:145
  152.8 2.0 %bitcast_convert_fusion = bf16[4,4,64,2,256]{4,1,3,2,0:T(4,128)(2,1)} fusion(bf16[8,2,64,2,256]{4,1,3,2,0:T(2,128)(2,1)S(1)} %all-to-all-done, pred[4,8,2]{1,0,2:T(4,128)(4,1)S(1)} %iota_compare_fusion.2, pred[4,8,2]{1,2,0:T(4,128)(4,1)S(1)} %broadcast_compare_fusion), kind=kOutput, calls=%fused_computation.1 | convolution fusion | flops 17301760 | bytes 2097280 | tf_op jit(solution)/shard_map/tkzp,zpxhw->tkxhw/dot_general | solution.py:161
  154.8 4.3 %all-to-all-start.1 = ((bf16[4,4,64,2,256]{4,1,3,2,0:T(4,128)(2,1)}), bf16[4,4,64,2,256]{4,1,3,2,0:T(4,128)(2,1)S(1)}, u32[]{:S(2)}, u32[]{:S(2)}) async-start(bf16[4,4,64,2,256]{4,1,3,2,0:T(4,128)(2,1)} %bitcast_convert_fusion), calls=%async_computation.1 | async-start | bytes 2097152 | tf_op jit(solution)/shard_map/all_to_all | solution.py:164
  159.4 0.7 copy-done.1
  160.5 0.7 copy-done.3
  161.5 1.0 copy.185
  162.5 10.1 %all-to-all-done.1 = bf16[4,4,64,2,256]{4,1,3,2,0:T(4,128)(2,1)S(1)} async-done(((bf16[4,4,64,2,256]{4,1,3,2,0:T(4,128)(2,1)}), bf16[4,4,64,2,256]{4,1,3,2,0:T(4,128)(2,1)S(1)}, u32[]{:S(2)}, u32[]{:S(2)}) %all-to-all-start.1) | async-done | bytes 1048608 | tf_op jit(solution)/shard_map/all_to_all | solution.py:164
  172.6 0.7 reduce_sum.62
  173.4 1.0 copy.186
  (63 shorter events, 6.8 us)
Async XLA Ops:
  1.6 24.8 %collective-permute-start = (bf16[128,2,256]{2,0,1:T(8,128)(2,1)S(1)}, bf16[128,2,256]{2,0,1:T(8,128)(2,1)S(1)}, u32[]{:S(2)}, u32[]{:S(2)}) collective-permute-start(bf16[128,2,256]{2,0,1:T(8,128)(2,1)S(1)} %bitcast.227), channel_id=1, source_target_pairs={{0,64},{64,128},{128,192},{192,256},{256,320},{320,384},{384,448},... | collective-permute-start | bytes 393224 | tf_op jit(solution)/shard_map/ppermute | solution.py:15
  16.9 10.1 %collective-permute-start.3 = (bf16[128,2,256]{2,0,1:T(8,128)(2,1)S(1)}, bf16[128,2,256]{2,0,1:T(8,128)(2,1)}, u32[]{:S(2)}, u32[]{:S(2)}) collective-permute-start(bf16[128,2,256]{2,0,1:T(8,128)(2,1)S(1)} %bitcast.228), channel_id=1, source_target_pairs={{128,384},{384,640},{640,896},{129,385},{385,641},{641,897},{130,3... | collective-permute-start | bytes 393224 | tf_op jit(solution)/shard_map/ppermute | solution.py:21
  18.3 10.9 %collective-permute-start.1 = (bf16[128,2,256]{2,0,1:T(8,128)(2,1)S(1)}, bf16[128,2,256]{2,0,1:T(8,128)(2,1)S(1)}, u32[]{:S(2)}, u32[]{:S(2)}) collective-permute-start(bf16[128,2,256]{2,0,1:T(8,128)(2,1)S(1)} %bitcast.229), channel_id=1, source_target_pairs={{0,128},{64,192},{256,384},{320,448},{512,640},{576,704},{768,896}... | collective-permute-start | bytes 393224 | tf_op jit(solution)/shard_map/ppermute | solution.py:21
  23.4 1.0 copy-start.4
  26.4 2.8 %collective-permute-start.2 = (bf16[128,2,256]{2,0,1:T(8,128)(2,1)S(1)}, bf16[128,2,256]{2,0,1:T(8,128)(2,1)S(1)}, u32[]{:S(2)}, u32[]{:S(2)}) collective-permute-start(bf16[128,2,256]{2,0,1:T(8,128)(2,1)S(1)} %collective-permute-done), channel_id=1, source_target_pairs={{256,320},{512,576},{768,832},{257,321},{513,577},{769,833},{258,3... | collective-permute-start | bytes 393224 | tf_op jit(solution)/shard_map/ppermute | solution.py:21
  27.1 2.8 %collective-permute-start.4 = (bf16[128,2,256]{2,0,1:T(8,128)(2,1)}, bf16[128,2,256]{2,0,1:T(8,128)(2,1)S(1)}, u32[]{:S(2)}, u32[]{:S(2)}) collective-permute-start(bf16[128,2,256]{2,0,1:T(8,128)(2,1)} %collective-permute-done.3), channel_id=1, source_target_pairs={{384,256},{640,512},{896,768},{385,257},{641,513},{897,769},{386,2... | collective-permute-start | bytes 393224 | tf_op jit(solution)/shard_map/ppermute | solution.py:21
  29.2 2.0 %copy-start.7 = (f32[2,8,128]{2,1,0:T(8,128)S(1)}, f32[2,8,128]{2,1,0:T(8,128)}, u32[]{:S(2)}) copy-start(f32[2,8,128]{2,1,0:T(8,128)} %get-tuple-element.23) | copy-start | bytes 24580
  29.2 2.0 %copy-start.5 = (bf16[1,128,2048]{1,2,0:T(8,128)(2,1)S(1)}, bf16[1,128,2048]{1,2,0:T(8,128)(2,1)}, u32[]{:S(2)}) copy-start(bf16[1,128,2048]{1,2,0:T(8,128)(2,1)} %copy.154) | copy-start | bytes 1572868
  29.2 0.7 copy-start.6
  32.2 0.8 copy-start
  33.3 6.8 %copy-start.2 = (bf16[2,8,128,128]{2,3,1,0:T(8,128)(2,1)}, bf16[2,8,128,128]{2,3,1,0:T(8,128)(2,1)S(1)}, u32[]{:S(2)}) copy-start(bf16[2,8,128,128]{2,3,1,0:T(8,128)(2,1)S(1)} %fusion.23) | copy-start | bytes 1572868
  33.9 13.9 %collective-permute-start.5 = (bf16[128,2,256]{0,2,1:T(8,128)(2,1)S(1)}, bf16[128,2,256]{0,2,1:T(8,128)(2,1)S(1)}, u32[]{:S(2)}, u32[]{:S(2)}) collective-permute-start(bf16[128,2,256]{0,2,1:T(8,128)(2,1)S(1)} %fusion.62), channel_id=1, source_target_pairs={{64,0},{128,64},{192,128},{320,256},{384,320},{448,384},{576,512},... | collective-permute-start | bytes 393224 | tf_op jit(solution)/shard_map/ppermute | solution.py:21
  39.5 1.3 collective-permute-start.6
  40.8 45.7 %collective-permute-start.7 = (bf16[128,2,256]{0,2,1:T(8,128)(2,1)S(1)}, bf16[128,2,256]{0,2,1:T(8,128)(2,1)S(1)}, u32[]{:S(2)}, u32[]{:S(2)}) collective-permute-start(bf16[128,2,256]{0,2,1:T(8,128)(2,1)S(1)} %fusion.44), channel_id=1, source_target_pairs={{128,0},{192,64},{256,128},{320,192},{384,256},{448,320},{512,384}... | collective-permute-start | bytes 393224 | tf_op jit(solution)/shard_map/ppermute | solution.py:21
  88.6 13.0 %copy-start.8 = (s32[1,32,2]{1,2,0:T(2,128)S(1)}, s32[1,32,2]{1,2,0:T(2,128)}, u32[]{:S(2)}) copy-start(s32[1,32,2]{1,2,0:T(2,128)} %param.9) | copy-start | bytes 772
  88.6 64.2 %all-to-all-start = ((bf16[8,2,64,2,256]{4,1,3,2,0:T(2,128)(2,1)}), bf16[8,2,64,2,256]{4,1,3,2,0:T(2,128)(2,1)S(1)}, u32[]{:S(2)}, u32[]{:S(2)}) async-start(bf16[8,2,64,2,256]{4,1,3,2,0:T(2,128)(2,1)} %multiply_bitcast_fusion), calls=%async_computation | async-start | bytes 2097152 | tf_op jit(solution)/shard_map/all_to_all | solution.py:145
  154.8 17.8 %all-to-all-start.1 = ((bf16[4,4,64,2,256]{4,1,3,2,0:T(4,128)(2,1)}), bf16[4,4,64,2,256]{4,1,3,2,0:T(4,128)(2,1)S(1)}, u32[]{:S(2)}, u32[]{:S(2)}) async-start(bf16[4,4,64,2,256]{4,1,3,2,0:T(4,128)(2,1)} %bitcast_convert_fusion), calls=%async_computation.1 | async-start | bytes 2097152 | tf_op jit(solution)/shard_map/all_to_all | solution.py:164
  159.1 1.0 copy-start.1
  160.1 1.0 copy-start.3

commit v5 on v3

--- a/solution.py
+++ b/solution.py
@@ -43,63 +43,52 @@
         relay = [(d - 1, d) for d in range(2, blocks) if near[d - 1][d] and not near[d - 2][d - 1]]
         direct = [(d - 2, d) for d in range(2, blocks) if (d - 1, d) not in relay]
         kv_blocks.append(moved(kv_local, "ctx", direct) + moved(kv_blocks[1], "ctx", relay))
-    totals = jnp.zeros((kv_heads, group_size, tok_rows), jnp.float32)
-    out_acc = jnp.zeros((tok_rows, kv_heads, group_size, HD), jnp.float32)
-    saved_exp = []
+    window = jnp.concatenate(kv_blocks, 0)
+    key_window = window[..., :HD]
+    value_window = window[..., HD:]
+    seen_parts = []
     for distance in range(reach_steps):
-        scores = (
-            jnp.einsum(
-                "igad,jgd->gaij",
-                query_four,
-                kv_blocks[distance][..., :HD],
-                preferred_element_type=jnp.float32,
-            )
-            * scale_factor
-        )
         source = ctx_index - distance
         key_pos = source * tok_rows + offsets
         key_doc = lax.dynamic_slice_in_dim(doc_row, jnp.maximum(source, 0) * tok_rows, tok_rows, 0)
-        exp_scores = jnp.where(
-            (
-                (query_doc[:, None] == key_doc[None, :])
-                & (key_pos[None, :] <= query_pos[:, None])
-                & (key_pos[None, :] >= 0)
-            )[None, None],
-            jnp.exp(scores),
-            0.0,
+        seen_parts.append(
+            (query_doc[:, None] == key_doc[None, :])
+            & (key_pos[None, :] <= query_pos[:, None])
+            & (key_pos[None, :] >= 0)
         )
-        saved_exp.append(exp_scores)
-        totals = totals + jnp.sum(exp_scores, -1)
-        out_acc = out_acc + jnp.einsum(
-            "gaij,jgd->igad",
-            exp_scores.astype(jnp.bfloat16),
-            kv_blocks[distance][..., HD:],
-            preferred_element_type=jnp.float32,
-        )
+    seen = jnp.concatenate(seen_parts, 1)
+    scores = (
+        jnp.einsum("igad,jgd->gaij", query_four, key_window, preferred_element_type=jnp.float32)
+        * scale_factor
+    )
+    exp_scores = jnp.where(seen[None, None], jnp.exp(scores), 0.0)
+    totals = jnp.sum(exp_scores, -1)
+    out_acc = jnp.einsum(
+        "gaij,jgd->igad",
+        exp_scores.astype(jnp.bfloat16),
+        value_window,
+        preferred_element_type=jnp.float32,
+    )
     attended = out_acc / jnp.transpose(totals, (2, 0, 1))[..., None]
     delta = jnp.transpose(jnp.sum(grad_four.astype(jnp.float32) * attended, -1), (1, 2, 0))
-    dq_acc = jnp.zeros((tok_rows, kv_heads, group_size, HD), jnp.float32)
-    terms = []
-    for distance in range(reach_steps):
-        key_block = kv_blocks[distance][..., :HD]
-        value_block = kv_blocks[distance][..., HD:]
-        probs = saved_exp[distance] / totals[..., None]
-        probs_low = probs.astype(jnp.bfloat16)
-        grad_probs = jnp.einsum(
-            "igad,jgd->gaij", grad_four, value_block, preferred_element_type=jnp.float32
-        )
-        score_low = (probs * (grad_probs - delta[..., None])).astype(jnp.bfloat16)
-        dq_acc = dq_acc + jnp.einsum(
-            "gaij,jgd->igad", score_low, key_block, preferred_element_type=jnp.float32
-        )
-        key_grad = (
-            jnp.einsum("gaij,igad->jgd", score_low, query_four, preferred_element_type=jnp.float32)
-            * scale_factor
-        )
-        value_grad = jnp.einsum(
-            "gaij,igad->jgd", probs_low, grad_four, preferred_element_type=jnp.float32
-        )
-        terms.append(jnp.concatenate([key_grad, value_grad], -1))
+    probs = exp_scores / totals[..., None]
+    probs_low = probs.astype(jnp.bfloat16)
+    grad_probs = jnp.einsum(
+        "igad,jgd->gaij", grad_four, value_window, preferred_element_type=jnp.float32
+    )
+    score_low = (probs * (grad_probs - delta[..., None])).astype(jnp.bfloat16)
+    dq_acc = jnp.einsum(
+        "gaij,jgd->igad", score_low, key_window, preferred_element_type=jnp.float32
+    )
+    key_grad = (
+        jnp.einsum("gaij,igad->jgd", score_low, query_four, preferred_element_type=jnp.float32)
+        * scale_factor
+    )
+    value_grad = jnp.einsum(
+        "gaij,igad->jgd", probs_low, grad_four, preferred_element_type=jnp.float32
+    )
+    both = jnp.concatenate([key_grad, value_grad], -1)
+    terms = [both[d * tok_rows:(d + 1) * tok_rows] for d in range(reach_steps)]
     kv_sum = terms[0]
     if reach_steps == 2:
         kv_sum = kv_sum + shifted(terms[1].astype(jnp.bfloat16), "ctx", -1).astype(jnp.float32)

time: 170 us -> 166 us (0.976)
  the two profiles are of different devices: /device:TPU:16 before, /device:TPU:24 now
where the time goes in v5:
time: 166 us; the launch traced here: 163 us
  waiting for transfers between devices  88.7 us (53%)
  starting transfers between devices  54.8 us (33%)
  local copies, waits for them, and re-layouts  7.75 us (5%)
  matrix products  7.53 us (5%)
  other arithmetic  3.37 us (2%)
    all_to_all x1, waiting for transfers between devices, shards(): lax.all_to_all(first_out, 'sz', split_axis=0, concat_axis=0, tiled=True)  48.9 us
    ppermute x5, waiting for transfers between devices, moved(): return lax.ppermute(shard, axis, pairs)  29.7 us
    all_to_all x1, starting transfers between devices, shards(): lax.all_to_all(first_out, 'sz', split_axis=0, concat_axis=0, tiled=True)  27.1 us
    ppermute x1, starting transfers between devices, shifted(): return lax.ppermute(shard, axis, pairs)  15.4 us
    all_to_all x1, waiting for transfers between devices, shards(): lax.all_to_all(second_out, 'sx', split_axis=0, concat_axis=0, tiled=True)  9.39 us
    ppermute x5, starting transfers between devices, moved(): return lax.ppermute(shard, axis, pairs)  7.96 us
    all_to_all x1, starting transfers between devices, shards(): lax.all_to_all(second_out, 'sx', split_axis=0, concat_axis=0, tiled=True)  4.32 us
    unnamed x8, local copies, waits for them, and re-layouts  4.23 us
  transfers between devices with their start and end apart: 8, of which 5 were waited for; matrix products, arithmetic and copies ran while one was open for 4% of the time, Pallas kernels for 0%

profile of v5, /device:TPU:24, one launch (start us, length us, event | category | flops | bytes accessed | tf_op | source)
XLA Modules:
  0.0 163.0 jit_solution(9483971161141691342)
XLA Ops:
  0.6 0.9 copy.120
  1.6 15.4 %collective-permute-start = (bf16[128,2,256]{2,0,1:T(8,128)(2,1)S(1)}, bf16[128,2,256]{2,0,1:T(8,128)(2,1)S(1)}, u32[]{:S(2)}, u32[]{:S(2)}) collective-permute-start(bf16[128,2,256]{2,0,1:T(8,128)(2,1)S(1)} %bitcast.127), channel_id=1, source_target_pairs={{0,64},{64,128},{128,192},{192,256},{256,320},{320,384},{384,448},... | collective-permute-start | bytes 393224 | tf_op jit(solution)/shard_map/ppermute | solution.py:15
  16.9 1.3 collective-permute-start.1
  18.3 0.7 fusion.53
  19.1 0.7 collective-permute-done
  19.7 0.7 collective-permute-start.2
  20.4 0.2 and_and_fusion.2
  20.6 1.3 copy.114
  21.9 1.3 copy.80
  23.3 2.0 %collective-permute-done.1 = bf16[128,2,256]{2,0,1:T(8,128)(2,1)S(1)} collective-permute-done((bf16[128,2,256]{2,0,1:T(8,128)(2,1)S(1)}, bf16[128,2,256]{2,0,1:T(8,128)(2,1)S(1)}, u32[]{:S(2)}, u32[]{:S(2)}) %collective-permute-start.1) | collective-permute-done | bytes 131104 | tf_op jit(solution)/shard_map/ppermute | solution.py:21
  25.4 0.8 fusion.4
  26.2 0.9 fusion.16
  27.1 0.7 fusion.27
  27.8 2.1 %fusion.1 = bf16[2,8,128,384]{2,3,1,0:T(8,128)(2,1)S(1)} fusion(bf16[128,2,8,128]{0,3,2,1:T(8,128)(2,1)} %bitcast.125, f32[2,8,128]{2,1,0:T(8,128)S(1)} %bitcast.132, f32[2,8,128]{2,1,0:T(8,128)S(1)} %get-tuple-element.23, f32[2,384,128,8]{2,1,3,0:T(8,128)S(1)} %get-tuple-element.24, pred[128,384]{0,1:T(8,128)(4,1)S(1)} %pad_add_fusion, ...), kind=kOutput, calls=%fused_computation.3 | convolution fusion | flops 206045184 | bytes 5505024 | tf_op jit(solution)/shard_map/igad,jgd->gaij/dot_general | solution.py:76
  29.9 0.6 fusion.20
  30.5 0.7 collective-permute-start.4
  31.2 0.2 fusion.47
  31.4 2.3 %collective-permute-start.3 = (bf16[128,2,256]{0,2,1:T(8,128)(2,1)S(1)}, bf16[128,2,256]{0,2,1:T(8,128)(2,1)S(1)}, u32[]{:S(2)}, u32[]{:S(2)}) collective-permute-start(bf16[128,2,256]{0,2,1:T(8,128)(2,1)S(1)} %get-tuple-element.14), channel_id=1, source_target_pairs={{64,0},{128,64},{192,128},{320,256},{384,320},{448,384},{576,512},... | collective-permute-start | bytes 393224 | tf_op jit(solution)/shard_map/ppermute | solution.py:21
  33.8 3.0 %collective-permute-start.5 = (bf16[128,2,256]{0,2,1:T(8,128)(2,1)S(1)}, bf16[128,2,256]{0,2,1:T(8,128)(2,1)S(1)}, u32[]{:S(2)}, u32[]{:S(2)}) collective-permute-start(bf16[128,2,256]{0,2,1:T(8,128)(2,1)S(1)} %fusion.39), channel_id=1, source_target_pairs={{128,0},{192,64},{256,128},{320,192},{384,256},{448,320},{512,384}... | collective-permute-start | bytes 393224 | tf_op jit(solution)/shard_map/ppermute | solution.py:21
  36.8 27.7 %collective-permute-done.5 = bf16[128,2,256]{0,2,1:T(8,128)(2,1)S(1)} collective-permute-done((bf16[128,2,256]{0,2,1:T(8,128)(2,1)S(1)}, bf16[128,2,256]{0,2,1:T(8,128)(2,1)S(1)}, u32[]{:S(2)}, u32[]{:S(2)}) %collective-permute-start.5) | collective-permute-done | bytes 131104 | tf_op jit(solution)/shard_map/ppermute | solution.py:21
  64.7 0.1 copy.92
  64.8 1.8 %multiply_bitcast_fusion = bf16[8,2,64,2,256]{4,1,3,2,0:T(2,128)(2,1)} fusion(bf16[2,8]{0,1:T(8,128)(2,1)S(1)} %fusion.46, bf16[2,64,2,256]{3,0,2,1:T(2,128)(2,1)S(1)} %copy.92), kind=kLoop, calls=%fused_computation.27 | loop fusion | flops 524288 | bytes 1179680 | tf_op jit(solution)/shard_map/cp,pxhw->cpxhw/transpose | solution.py:122
  66.6 27.1 %all-to-all-start = ((bf16[8,2,64,2,256]{4,1,3,2,0:T(2,128)(2,1)}), bf16[8,2,64,2,256]{4,1,3,2,0:T(2,128)(2,1)S(1)}, u32[]{:S(2)}, u32[]{:S(2)}) async-start(bf16[8,2,64,2,256]{4,1,3,2,0:T(2,128)(2,1)} %multiply_bitcast_fusion), calls=%async_computation | async-start | bytes 2097152 | tf_op jit(solution)/shard_map/all_to_all | solution.py:125
  94.1 0.6 gather_fusion
  95.1 48.9 %all-to-all-done = bf16[8,2,64,2,256]{4,1,3,2,0:T(2,128)(2,1)S(1)} async-done(((bf16[8,2,64,2,256]{4,1,3,2,0:T(2,128)(2,1)}), bf16[8,2,64,2,256]{4,1,3,2,0:T(2,128)(2,1)S(1)}, u32[]{:S(2)}, u32[]{:S(2)}) %all-to-all-start) | async-done | bytes 1048608 | tf_op jit(solution)/shard_map/all_to_all | solution.py:125
  144.1 2.0 %bitcast_convert_fusion = bf16[4,4,64,2,256]{4,1,3,2,0:T(4,128)(2,1)} fusion(bf16[8,2,64,2,256]{4,1,3,2,0:T(2,128)(2,1)S(1)} %all-to-all-done, pred[4,8,2]{1,0,2:T(4,128)(4,1)S(1)} %iota_compare_fusion.2, pred[4,8,2]{1,2,0:T(4,128)(4,1)S(1)} %broadcast_compare_fusion), kind=kOutput, calls=%fused_computation.5 | convolution fusion | flops 17301760 | bytes 2097280 | tf_op jit(solution)/shard_map/tkzp,zpxhw->tkxhw/dot_general | solution.py:141
  146.1 4.3 %all-to-all-start.1 = ((bf16[4,4,64,2,256]{4,1,3,2,0:T(4,128)(2,1)}), bf16[4,4,64,2,256]{4,1,3,2,0:T(4,128)(2,1)S(1)}, u32[]{:S(2)}, u32[]{:S(2)}) async-start(bf16[4,4,64,2,256]{4,1,3,2,0:T(4,128)(2,1)} %bitcast_convert_fusion), calls=%async_computation.1 | async-start | bytes 2097152 | tf_op jit(solution)/shard_map/all_to_all | solution.py:144
  150.4 0.5 fusion.15
  150.9 1.0 copy.95
  151.9 9.4 %all-to-all-done.1 = bf16[4,4,64,2,256]{4,1,3,2,0:T(4,128)(2,1)S(1)} async-done(((bf16[4,4,64,2,256]{4,1,3,2,0:T(4,128)(2,1)}), bf16[4,4,64,2,256]{4,1,3,2,0:T(4,128)(2,1)S(1)}, u32[]{:S(2)}, u32[]{:S(2)}) %all-to-all-start.1) | async-done | bytes 1048608 | tf_op jit(solution)/shard_map/all_to_all | solution.py:144
  161.3 0.7 reduce_sum.42
  162.0 1.0 copy.96
  (33 shorter events, 1.1 us)
Async XLA Ops:
  1.6 18.2 %collective-permute-start = (bf16[128,2,256]{2,0,1:T(8,128)(2,1)S(1)}, bf16[128,2,256]{2,0,1:T(8,128)(2,1)S(1)}, u32[]{:S(2)}, u32[]{:S(2)}) collective-permute-start(bf16[128,2,256]{2,0,1:T(8,128)(2,1)S(1)} %bitcast.127), channel_id=1, source_target_pairs={{0,64},{64,128},{128,192},{192,256},{256,320},{320,384},{384,448},... | collective-permute-start | bytes 393224 | tf_op jit(solution)/shard_map/ppermute | solution.py:15
  16.9 8.4 %collective-permute-start.1 = (bf16[128,2,256]{2,0,1:T(8,128)(2,1)S(1)}, bf16[128,2,256]{2,0,1:T(8,128)(2,1)S(1)}, u32[]{:S(2)}, u32[]{:S(2)}) collective-permute-start(bf16[128,2,256]{2,0,1:T(8,128)(2,1)S(1)} %bitcast.128), channel_id=1, source_target_pairs={{0,128},{64,192},{128,256},{256,384},{320,448},{384,512},{512,640}... | collective-permute-start | bytes 393224 | tf_op jit(solution)/shard_map/ppermute | solution.py:21
  19.7 5.6 %collective-permute-start.2 = (bf16[128,2,256]{2,0,1:T(8,128)(2,1)S(1)}, bf16[128,2,256]{2,0,1:T(8,128)(2,1)S(1)}, u32[]{:S(2)}, u32[]{:S(2)}) collective-permute-start(bf16[128,2,256]{2,0,1:T(8,128)(2,1)S(1)} %collective-permute-done), channel_id=1, source_target_pairs={{256,320},{512,576},{768,832},{257,321},{513,577},{769,833},{258,3... | collective-permute-start | bytes 393224 | tf_op jit(solution)/shard_map/ppermute | solution.py:21
  23.3 3.8 %copy-start = (bf16[1,128,2048]{1,2,0:T(8,128)(2,1)}, bf16[1,128,2048]{1,2,0:T(8,128)(2,1)S(1)}, u32[]{:S(2)}) copy-start(bf16[1,128,2048]{1,2,0:T(8,128)(2,1)S(1)} %copy.80) | copy-start | bytes 1572868
  29.9 1.4 copy-start.1
  30.5 3.2 %collective-permute-start.4 = (f32[128,2,256]{0,2,1:T(8,128)S(1)}, f32[128,2,256]{0,2,1:T(8,128)S(1)}, u32[]{:S(2)}, u32[]{:S(2)}) collective-permute-start(f32[128,2,256]{0,2,1:T(8,128)S(1)} %get-tuple-element.15), channel_id=1, source_target_pairs={{256,320},{512,576},{768,832},{257,321},{513,577},{769,833},{258,3... | collective-permute-start | bytes 786440 | tf_op jit(solution)/shard_map/ppermute | solution.py:21
  31.4 5.4 %collective-permute-start.3 = (bf16[128,2,256]{0,2,1:T(8,128)(2,1)S(1)}, bf16[128,2,256]{0,2,1:T(8,128)(2,1)S(1)}, u32[]{:S(2)}, u32[]{:S(2)}) collective-permute-start(bf16[128,2,256]{0,2,1:T(8,128)(2,1)S(1)} %get-tuple-element.14), channel_id=1, source_target_pairs={{64,0},{128,64},{192,128},{320,256},{384,320},{448,384},{576,512},... | collective-permute-start | bytes 393224 | tf_op jit(solution)/shard_map/ppermute | solution.py:21
  33.8 30.7 %collective-permute-start.5 = (bf16[128,2,256]{0,2,1:T(8,128)(2,1)S(1)}, bf16[128,2,256]{0,2,1:T(8,128)(2,1)S(1)}, u32[]{:S(2)}, u32[]{:S(2)}) collective-permute-start(bf16[128,2,256]{0,2,1:T(8,128)(2,1)S(1)} %fusion.39), channel_id=1, source_target_pairs={{128,0},{192,64},{256,128},{320,192},{384,256},{448,320},{512,384}... | collective-permute-start | bytes 393224 | tf_op jit(solution)/shard_map/ppermute | solution.py:21
  66.6 77.4 %all-to-all-start = ((bf16[8,2,64,2,256]{4,1,3,2,0:T(2,128)(2,1)}), bf16[8,2,64,2,256]{4,1,3,2,0:T(2,128)(2,1)S(1)}, u32[]{:S(2)}, u32[]{:S(2)}) async-start(bf16[8,2,64,2,256]{4,1,3,2,0:T(2,128)(2,1)} %multiply_bitcast_fusion), calls=%async_computation | async-start | bytes 2097152 | tf_op jit(solution)/shard_map/all_to_all | solution.py:125
  146.1 15.2 %all-to-all-start.1 = ((bf16[4,4,64,2,256]{4,1,3,2,0:T(4,128)(2,1)}), bf16[4,4,64,2,256]{4,1,3,2,0:T(4,128)(2,1)S(1)}, u32[]{:S(2)}, u32[]{:S(2)}) async-start(bf16[4,4,64,2,256]{4,1,3,2,0:T(4,128)(2,1)} %bitcast_convert_fusion), calls=%async_computation.1 | async-start | bytes 2097152 | tf_op jit(solution)/shard_map/all_to_all | solution.py:144

commit v6 on v5

--- a/solution.py
+++ b/solution.py
@@ -141,8 +141,12 @@
     second_out = jnp.einsum(
         "tkzp,zpxhw->tkxhw", second_map, first_in, preferred_element_type=jnp.float32
     ).astype(jnp.bfloat16)
-    second_in = lax.all_to_all(second_out, "sx", split_axis=0, concat_axis=0, tiled=True)
-    owned = jnp.sum(second_in.astype(jnp.float32), 0).astype(jnp.bfloat16)
+    owned_sum = lax.dynamic_index_in_dim(second_out, row_index, 0, keepdims=False).astype(jnp.float32)
+    for step in range(1, outer):
+        outbound = lax.dynamic_index_in_dim(second_out, (row_index + step) % outer, 0, keepdims=False)
+        inbound = lax.ppermute(outbound, "sx", [(i, (i + step) % outer) for i in range(outer)])
+        owned_sum = owned_sum + inbound.astype(jnp.float32)
+    owned = owned_sum.astype(jnp.bfloat16)
     return (query_grad, owned.reshape(1, 2 * piece_count * PIECE, kv_heads, 2 * HD))
 
 

time: 166 us -> 170 us (1.024)
  starting transfers between devices: 54.8 us -> 61.8 us
  waiting for transfers between devices: 88.7 us -> 83.1 us
    ppermute x0 -> x3, starting transfers between devices: none -> 11.4 us  [shards(): lax.ppermute(outbound, 'sx', [(i, (i + step) % outer) for i in range(oute...]
    all_to_all x1 -> x0, waiting for transfers between devices: 9.39 us -> none  [shards(): lax.all_to_all(second_out, 'sx', split_axis=0, concat_axis=0, tiled=True)]
    all_to_all x1 -> x0, starting transfers between devices: 4.32 us -> none  [shards(): lax.all_to_all(second_out, 'sx', split_axis=0, concat_axis=0, tiled=True)]
    ppermute x0 -> x3, waiting for transfers between devices: none -> 3.65 us  [shards(): lax.ppermute(outbound, 'sx', [(i, (i + step) % outer) for i in range(oute...]
  transfers between devices with their start and end apart: 8 -> 10, of which waited for: 5 -> 6; matrix products, arithmetic and copies ran while one was open for 4% -> 4% of each run, Pallas kernels for 0% -> 0%
where the time goes in v6:
time: 170 us; the launch traced here: 167 us
  waiting for transfers between devices  83.1 us (49%)
  starting transfers between devices  61.8 us (36%)
  local copies, waits for them, and re-layouts  8.81 us (5%)
  matrix products  7.77 us (5%)
  other arithmetic  4.1 us (2%)
    all_to_all x1, waiting for transfers between devices, shards(): lax.all_to_all(first_out, 'sz', split_axis=0, concat_axis=0, tiled=True)  49.1 us
    ppermute x5, waiting for transfers between devices, moved(): return lax.ppermute(shard, axis, pairs)  29.7 us
    all_to_all x1, starting transfers between devices, shards(): lax.all_to_all(first_out, 'sz', split_axis=0, concat_axis=0, tiled=True)  27.1 us
    ppermute x1, starting transfers between devices, shifted(): return lax.ppermute(shard, axis, pairs)  15.4 us
    ppermute x3, starting transfers between devices, shards(): lax.ppermute(outbound, 'sx', [(i, (i + step) % outer) for i in range(oute...  11.4 us
    ppermute x5, starting transfers between devices, moved(): return lax.ppermute(shard, axis, pairs)  7.96 us
    unnamed x8, local copies, waits for them, and re-layouts  4.23 us
    ppermute x3, waiting for transfers between devices, shards(): lax.ppermute(outbound, 'sx', [(i, (i + step) % outer) for i in range(oute...  3.65 us
  transfers between devices with their start and end apart: 10, of which 6 were waited for; matrix products, arithmetic and copies ran while one was open for 4% of the time, Pallas kernels for 0%

profile of v6, /device:TPU:24, one launch (start us, length us, event | category | flops | bytes accessed | tf_op | source)
XLA Modules:
  0.0 166.5 jit_solution(469050913255660518)
XLA Ops:
  0.6 0.9 copy.104
  1.6 15.4 %collective-permute-start = (bf16[128,2,256]{2,0,1:T(8,128)(2,1)S(1)}, bf16[128,2,256]{2,0,1:T(8,128)(2,1)S(1)}, u32[]{:S(2)}, u32[]{:S(2)}) collective-permute-start(bf16[128,2,256]{2,0,1:T(8,128)(2,1)S(1)} %bitcast.136), channel_id=1, source_target_pairs={{0,64},{64,128},{128,192},{192,256},{256,320},{320,384},{384,448},... | collective-permute-start | bytes 393224 | tf_op jit(solution)/shard_map/ppermute | solution.py:15
  16.9 1.3 collective-permute-start.1
  18.3 0.7 fusion.57
  19.1 0.7 collective-permute-done
  19.7 0.7 collective-permute-start.2
  20.6 1.3 copy.98
  21.9 1.3 copy.64
  23.3 2.0 %collective-permute-done.1 = bf16[128,2,256]{2,0,1:T(8,128)(2,1)S(1)} collective-permute-done((bf16[128,2,256]{2,0,1:T(8,128)(2,1)S(1)}, bf16[128,2,256]{2,0,1:T(8,128)(2,1)S(1)}, u32[]{:S(2)}, u32[]{:S(2)}) %collective-permute-start.1) | collective-permute-done | bytes 131104 | tf_op jit(solution)/shard_map/ppermute | solution.py:21
  25.4 0.8 fusion.4
  26.2 0.9 fusion.16
  27.1 0.7 fusion.27
  27.8 2.1 %fusion.1 = bf16[2,8,128,384]{2,3,1,0:T(8,128)(2,1)S(1)} fusion(bf16[128,2,8,128]{0,3,2,1:T(8,128)(2,1)} %bitcast.134, f32[2,8,128]{2,1,0:T(8,128)S(1)} %bitcast.141, f32[2,8,128]{2,1,0:T(8,128)S(1)} %get-tuple-element.24, f32[2,384,128,8]{2,1,3,0:T(8,128)S(1)} %get-tuple-element.25, pred[128,384]{0,1:T(8,128)(4,1)S(1)} %pad_add_fusion, ...), kind=kOutput, calls=%fused_computation.3 | convolution fusion | flops 206045184 | bytes 5505024 | tf_op jit(solution)/shard_map/igad,jgd->gaij/dot_general | solution.py:76
  29.9 0.6 fusion.20
  30.5 0.7 collective-permute-start.4
  31.4 2.3 %collective-permute-start.3 = (bf16[128,2,256]{0,2,1:T(8,128)(2,1)S(1)}, bf16[128,2,256]{0,2,1:T(8,128)(2,1)S(1)}, u32[]{:S(2)}, u32[]{:S(2)}) collective-permute-start(bf16[128,2,256]{0,2,1:T(8,128)(2,1)S(1)} %get-tuple-element.12), channel_id=1, source_target_pairs={{64,0},{128,64},{192,128},{320,256},{384,320},{448,384},{576,512},... | collective-permute-start | bytes 393224 | tf_op jit(solution)/shard_map/ppermute | solution.py:21
  33.8 3.0 %collective-permute-start.5 = (bf16[128,2,256]{0,2,1:T(8,128)(2,1)S(1)}, bf16[128,2,256]{0,2,1:T(8,128)(2,1)S(1)}, u32[]{:S(2)}, u32[]{:S(2)}) collective-permute-start(bf16[128,2,256]{0,2,1:T(8,128)(2,1)S(1)} %fusion.42), channel_id=1, source_target_pairs={{128,0},{192,64},{256,128},{320,192},{384,256},{448,320},{512,384}... | collective-permute-start | bytes 393224 | tf_op jit(solution)/shard_map/ppermute | solution.py:21
  36.8 27.7 %collective-permute-done.5 = bf16[128,2,256]{0,2,1:T(8,128)(2,1)S(1)} collective-permute-done((bf16[128,2,256]{0,2,1:T(8,128)(2,1)S(1)}, bf16[128,2,256]{0,2,1:T(8,128)(2,1)S(1)}, u32[]{:S(2)}, u32[]{:S(2)}) %collective-permute-start.5) | collective-permute-done | bytes 131104 | tf_op jit(solution)/shard_map/ppermute | solution.py:21
  64.8 1.9 %multiply_bitcast_fusion = bf16[8,2,64,2,256]{4,1,3,2,0:T(2,128)(2,1)} fusion(bf16[2,8]{0,1:T(8,128)(2,1)S(1)} %fusion.49, bf16[2,64,2,256]{3,0,2,1:T(2,128)(2,1)S(1)} %copy.76), kind=kLoop, calls=%fused_computation.27 | loop fusion | flops 524288 | bytes 1179680 | tf_op jit(solution)/shard_map/cp,pxhw->cpxhw/transpose | solution.py:122
  66.7 27.1 %all-to-all-start = ((bf16[8,2,64,2,256]{4,1,3,2,0:T(2,128)(2,1)}), bf16[8,2,64,2,256]{4,1,3,2,0:T(2,128)(2,1)}, u32[]{:S(2)}, u32[]{:S(2)}) async-start(bf16[8,2,64,2,256]{4,1,3,2,0:T(2,128)(2,1)} %multiply_bitcast_fusion), calls=%async_computation | async-start | bytes 2097152 | tf_op jit(solution)/shard_map/all_to_all | solution.py:125
  94.2 0.6 gather_fusion
  95.1 49.1 %all-to-all-done = bf16[8,2,64,2,256]{4,1,3,2,0:T(2,128)(2,1)} async-done(((bf16[8,2,64,2,256]{4,1,3,2,0:T(2,128)(2,1)}), bf16[8,2,64,2,256]{4,1,3,2,0:T(2,128)(2,1)}, u32[]{:S(2)}, u32[]{:S(2)}) %all-to-all-start) | async-done | bytes 1048608 | tf_op jit(solution)/shard_map/all_to_all | solution.py:125
  144.2 2.3 %bitcast_convert_fusion = bf16[4,4,64,2,256]{4,1,3,2,0:T(4,128)(2,1)S(1)} fusion(bf16[8,2,64,2,256]{4,1,3,2,0:T(2,128)(2,1)} %all-to-all-done, pred[4,8,2]{1,0,2:T(4,128)(4,1)S(1)} %iota_compare_fusion.2, pred[4,8,2]{1,2,0:T(4,128)(4,1)S(1)} %broadcast_compare_fusion), kind=kOutput, calls=%fused_computation.5 | convolution fusion | flops 17301760 | bytes 2097280 | tf_op jit(solution)/shard_map/tkzp,zpxhw->tkxhw/dot_general | solution.py:141
  146.5 1.1 dynamic-slice_bitcast_fusion.2
  147.5 3.4 %collective-permute-start.6 = (bf16[4,64,2,256]{3,0,2,1:T(4,128)(2,1)}, bf16[4,64,2,256]{3,0,2,1:T(4,128)(2,1)}, u32[]{:S(2)}, u32[]{:S(2)}) collective-permute-start(bf16[4,64,2,256]{3,0,2,1:T(4,128)(2,1)} %get-tuple-element.14), channel_id=1, source_target_pairs={{0,16},{16,32},{32,48},{48,0},{1,17},{17,33},{33,49},{49,1},{2,18}... | collective-permute-start | bytes 786440 | tf_op jit(solution)/shard_map/ppermute | solution.py:147
  151.0 4.6 %collective-permute-start.7 = (bf16[4,64,2,256]{3,0,2,1:T(4,128)(2,1)}, bf16[4,64,2,256]{3,0,2,1:T(4,128)(2,1)}, u32[]{:S(2)}, u32[]{:S(2)}) collective-permute-start(bf16[4,64,2,256]{3,0,2,1:T(4,128)(2,1)} %get-tuple-element.16), channel_id=1, source_target_pairs={{0,32},{16,48},{32,0},{48,16},{1,33},{17,49},{33,1},{49,17},{2,34}... | collective-permute-start | bytes 786440 | tf_op jit(solution)/shard_map/ppermute | solution.py:147
  155.5 3.4 %collective-permute-start.8 = (bf16[4,64,2,256]{3,0,2,1:T(4,128)(2,1)}, bf16[4,64,2,256]{3,0,2,1:T(4,128)(2,1)}, u32[]{:S(2)}, u32[]{:S(2)}) collective-permute-start(bf16[4,64,2,256]{3,0,2,1:T(4,128)(2,1)} %get-tuple-element.15), channel_id=1, source_target_pairs={{0,48},{16,0},{32,16},{48,32},{1,49},{17,1},{33,17},{49,33},{2,50}... | collective-permute-start | bytes 786440 | tf_op jit(solution)/shard_map/ppermute | solution.py:147
  159.5 1.0 copy.79
  160.5 0.6 collective-permute-done.7
  161.1 3.1 %collective-permute-done.8 = bf16[4,64,2,256]{3,0,2,1:T(4,128)(2,1)} collective-permute-done((bf16[4,64,2,256]{3,0,2,1:T(4,128)(2,1)}, bf16[4,64,2,256]{3,0,2,1:T(4,128)(2,1)}, u32[]{:S(2)}, u32[]{:S(2)}) %collective-permute-start.8) | collective-permute-done | bytes 262176 | tf_op jit(solution)/shard_map/ppermute | solution.py:147
  164.1 1.4 fusion.35
  165.6 1.0 copy.80
  (38 shorter events, 2.2 us)
Async XLA Ops:
  1.6 18.2 %collective-permute-start = (bf16[128,2,256]{2,0,1:T(8,128)(2,1)S(1)}, bf16[128,2,256]{2,0,1:T(8,128)(2,1)S(1)}, u32[]{:S(2)}, u32[]{:S(2)}) collective-permute-start(bf16[128,2,256]{2,0,1:T(8,128)(2,1)S(1)} %bitcast.136), channel_id=1, source_target_pairs={{0,64},{64,128},{128,192},{192,256},{256,320},{320,384},{384,448},... | collective-permute-start | bytes 393224 | tf_op jit(solution)/shard_map/ppermute | solution.py:15
  16.9 8.4 %collective-permute-start.1 = (bf16[128,2,256]{2,0,1:T(8,128)(2,1)S(1)}, bf16[128,2,256]{2,0,1:T(8,128)(2,1)S(1)}, u32[]{:S(2)}, u32[]{:S(2)}) collective-permute-start(bf16[128,2,256]{2,0,1:T(8,128)(2,1)S(1)} %bitcast.137), channel_id=1, source_target_pairs={{0,128},{64,192},{128,256},{256,384},{320,448},{384,512},{512,640}... | collective-permute-start | bytes 393224 | tf_op jit(solution)/shard_map/ppermute | solution.py:21
  19.7 5.6 %collective-permute-start.2 = (bf16[128,2,256]{2,0,1:T(8,128)(2,1)S(1)}, bf16[128,2,256]{2,0,1:T(8,128)(2,1)S(1)}, u32[]{:S(2)}, u32[]{:S(2)}) collective-permute-start(bf16[128,2,256]{2,0,1:T(8,128)(2,1)S(1)} %collective-permute-done), channel_id=1, source_target_pairs={{256,320},{512,576},{768,832},{257,321},{513,577},{769,833},{258,3... | collective-permute-start | bytes 393224 | tf_op jit(solution)/shard_map/ppermute | solution.py:21
  23.3 3.8 %copy-start = (bf16[1,128,2048]{1,2,0:T(8,128)(2,1)}, bf16[1,128,2048]{1,2,0:T(8,128)(2,1)S(1)}, u32[]{:S(2)}) copy-start(bf16[1,128,2048]{1,2,0:T(8,128)(2,1)S(1)} %copy.64) | copy-start | bytes 1572868
  29.9 1.4 copy-start.1
  30.5 3.2 %collective-permute-start.4 = (f32[128,2,256]{0,2,1:T(8,128)S(1)}, f32[128,2,256]{0,2,1:T(8,128)S(1)}, u32[]{:S(2)}, u32[]{:S(2)}) collective-permute-start(f32[128,2,256]{0,2,1:T(8,128)S(1)} %get-tuple-element.13), channel_id=1, source_target_pairs={{256,320},{512,576},{768,832},{257,321},{513,577},{769,833},{258,3... | collective-permute-start | bytes 786440 | tf_op jit(solution)/shard_map/ppermute | solution.py:21
  31.4 5.4 %collective-permute-start.3 = (bf16[128,2,256]{0,2,1:T(8,128)(2,1)S(1)}, bf16[128,2,256]{0,2,1:T(8,128)(2,1)S(1)}, u32[]{:S(2)}, u32[]{:S(2)}) collective-permute-start(bf16[128,2,256]{0,2,1:T(8,128)(2,1)S(1)} %get-tuple-element.12), channel_id=1, source_target_pairs={{64,0},{128,64},{192,128},{320,256},{384,320},{448,384},{576,512},... | collective-permute-start | bytes 393224 | tf_op jit(solution)/shard_map/ppermute | solution.py:21
  33.8 30.7 %collective-permute-start.5 = (bf16[128,2,256]{0,2,1:T(8,128)(2,1)S(1)}, bf16[128,2,256]{0,2,1:T(8,128)(2,1)S(1)}, u32[]{:S(2)}, u32[]{:S(2)}) collective-permute-start(bf16[128,2,256]{0,2,1:T(8,128)(2,1)S(1)} %fusion.42), channel_id=1, source_target_pairs={{128,0},{192,64},{256,128},{320,192},{384,256},{448,320},{512,384}... | collective-permute-start | bytes 393224 | tf_op jit(solution)/shard_map/ppermute | solution.py:21
  66.7 77.5 %all-to-all-start = ((bf16[8,2,64,2,256]{4,1,3,2,0:T(2,128)(2,1)}), bf16[8,2,64,2,256]{4,1,3,2,0:T(2,128)(2,1)}, u32[]{:S(2)}, u32[]{:S(2)}) async-start(bf16[8,2,64,2,256]{4,1,3,2,0:T(2,128)(2,1)} %multiply_bitcast_fusion), calls=%async_computation | async-start | bytes 2097152 | tf_op jit(solution)/shard_map/all_to_all | solution.py:125
  147.5 12.9 %collective-permute-start.6 = (bf16[4,64,2,256]{3,0,2,1:T(4,128)(2,1)}, bf16[4,64,2,256]{3,0,2,1:T(4,128)(2,1)}, u32[]{:S(2)}, u32[]{:S(2)}) collective-permute-start(bf16[4,64,2,256]{3,0,2,1:T(4,128)(2,1)} %get-tuple-element.14), channel_id=1, source_target_pairs={{0,16},{16,32},{32,48},{48,0},{1,17},{17,33},{33,49},{49,1},{2,18}... | collective-permute-start | bytes 786440 | tf_op jit(solution)/shard_map/ppermute | solution.py:147
  151.0 10.1 %collective-permute-start.7 = (bf16[4,64,2,256]{3,0,2,1:T(4,128)(2,1)}, bf16[4,64,2,256]{3,0,2,1:T(4,128)(2,1)}, u32[]{:S(2)}, u32[]{:S(2)}) collective-permute-start(bf16[4,64,2,256]{3,0,2,1:T(4,128)(2,1)} %get-tuple-element.16), channel_id=1, source_target_pairs={{0,32},{16,48},{32,0},{48,16},{1,33},{17,49},{33,1},{49,17},{2,34}... | collective-permute-start | bytes 786440 | tf_op jit(solution)/shard_map/ppermute | solution.py:147
  155.5 8.6 %collective-permute-start.8 = (bf16[4,64,2,256]{3,0,2,1:T(4,128)(2,1)}, bf16[4,64,2,256]{3,0,2,1:T(4,128)(2,1)}, u32[]{:S(2)}, u32[]{:S(2)}) collective-permute-start(bf16[4,64,2,256]{3,0,2,1:T(4,128)(2,1)} %get-tuple-element.15), channel_id=1, source_target_pairs={{0,48},{16,0},{32,16},{48,32},{1,49},{17,1},{33,17},{49,33},{2,50}... | collective-permute-start | bytes 786440 | tf_op jit(solution)/shard_map/ppermute | solution.py:147

commit v7 on v5

--- a/solution.py
+++ b/solution.py
@@ -57,8 +57,23 @@
             & (key_pos[None, :] >= 0)
         )
     seen = jnp.concatenate(seen_parts, 1)
+    own_scores = jnp.einsum(
+        "igad,jgd->gaij", query_four, kv_local[..., :HD], preferred_element_type=jnp.float32
+    )
+    own_grad_probs = jnp.einsum(
+        "igad,jgd->gaij", grad_four, kv_local[..., HD:], preferred_element_type=jnp.float32
+    )
+    far_window = jnp.concatenate(kv_blocks[1:], 0)
     scores = (
-        jnp.einsum("igad,jgd->gaij", query_four, key_window, preferred_element_type=jnp.float32)
+        jnp.concatenate(
+            [
+                own_scores,
+                jnp.einsum(
+                    "igad,jgd->gaij", query_four, far_window[..., :HD], preferred_element_type=jnp.float32
+                ),
+            ],
+            -1,
+        )
         * scale_factor
     )
     exp_scores = jnp.where(seen[None, None], jnp.exp(scores), 0.0)
@@ -73,8 +88,14 @@
     delta = jnp.transpose(jnp.sum(grad_four.astype(jnp.float32) * attended, -1), (1, 2, 0))
     probs = exp_scores / totals[..., None]
     probs_low = probs.astype(jnp.bfloat16)
-    grad_probs = jnp.einsum(
-        "igad,jgd->gaij", grad_four, value_window, preferred_element_type=jnp.float32
+    grad_probs = jnp.concatenate(
+        [
+            own_grad_probs,
+            jnp.einsum(
+                "igad,jgd->gaij", grad_four, far_window[..., HD:], preferred_element_type=jnp.float32
+            ),
+        ],
+        -1,
     )
     score_low = (probs * (grad_probs - delta[..., None])).astype(jnp.bfloat16)
     dq_acc = jnp.einsum(

time: 166 us -> 166 us (level)
  starting transfers between devices: 54.8 us -> 48.7 us
  waiting for transfers between devices: 88.7 us -> 94.2 us
    all_to_all x1, starting transfers between devices: 27.1 us -> 20.7 us  [shards(): lax.all_to_all(first_out, 'sz', split_axis=0, concat_axis=0, tiled=True)]
    ppermute x5, waiting for transfers between devices: 29.7 us -> 35.8 us  [moved(): return lax.ppermute(shard, axis, pairs)]
    unnamed x8 -> x14, local copies, waits for them, and re-layouts: 4.23 us -> 4.04 us
  transfers between devices with their start and end apart: 8 -> 8, of which waited for: 5 -> 4; matrix products, arithmetic and copies ran while one was open for 4% -> 4% of each run, Pallas kernels for 0% -> 0%
where the time goes in v7:
time: 166 us; the launch traced here: 163 us
  waiting for transfers between devices  94.2 us (57%)
  starting transfers between devices  48.7 us (29%)
  local copies, waits for them, and re-layouts  7.55 us (5%)
  matrix products  7.09 us (4%)
  other arithmetic  4.81 us (3%)
    all_to_all x1, waiting for transfers between devices, shards(): lax.all_to_all(first_out, 'sz', split_axis=0, concat_axis=0, tiled=True)  49 us
    ppermute x5, waiting for transfers between devices, moved(): return lax.ppermute(shard, axis, pairs)  35.8 us
    all_to_all x1, starting transfers between devices, shards(): lax.all_to_all(first_out, 'sz', split_axis=0, concat_axis=0, tiled=True)  20.7 us
    ppermute x1, starting transfers between devices, shifted(): return lax.ppermute(shard, axis, pairs)  15.4 us
    all_to_all x1, waiting for transfers between devices, shards(): lax.all_to_all(second_out, 'sx', split_axis=0, concat_axis=0, tiled=True)  9.38 us
    ppermute x5, starting transfers between devices, moved(): return lax.ppermute(shard, axis, pairs)  8.42 us
    all_to_all x1, starting transfers between devices, shards(): lax.all_to_all(second_out, 'sx', split_axis=0, concat_axis=0, tiled=True)  4.29 us
    unnamed x14, local copies, waits for them, and re-layouts  4.04 us
  transfers between devices with their start and end apart: 8, of which 4 were waited for; matrix products, arithmetic and copies ran while one was open for 4% of the time, Pallas kernels for 0%

profile of v7, /device:TPU:24, one launch (start us, length us, event | category | flops | bytes accessed | tf_op | source)
XLA Modules:
  0.0 163.3 jit_solution(8353403078746874985)
XLA Ops:
  0.6 1.0 copy.133
  1.6 15.4 %collective-permute-start = (bf16[128,2,256]{2,0,1:T(8,128)(2,1)S(1)}, bf16[128,2,256]{2,0,1:T(8,128)(2,1)S(1)}, u32[]{:S(2)}, u32[]{:S(2)}) collective-permute-start(bf16[128,2,256]{2,0,1:T(8,128)(2,1)S(1)} %bitcast.119), channel_id=1, source_target_pairs={{0,64},{64,128},{128,192},{192,256},{256,320},{320,384},{384,448},... | collective-permute-start | bytes 393224 | tf_op jit(solution)/shard_map/ppermute | solution.py:15
  17.0 1.3 collective-permute-start.1
  18.4 1.3 copy.127
  19.7 0.3 convolution_bitcast_fusion.3
  20.3 1.3 convolution_bitcast_fusion.2
  21.5 0.7 fusion.53
  22.3 0.7 collective-permute-start.2
  23.2 2.2 %collective-permute-done.1 = bf16[128,2,256]{2,0,1:T(8,128)(2,1)S(1)} collective-permute-done((bf16[128,2,256]{2,0,1:T(8,128)(2,1)S(1)}, bf16[128,2,256]{2,0,1:T(8,128)(2,1)S(1)}, u32[]{:S(2)}, u32[]{:S(2)}) %collective-permute-start.1) | collective-permute-done | bytes 131104 | tf_op jit(solution)/shard_map/ppermute | solution.py:21
  25.4 0.4 convolution_bitcast_fusion.1
  25.8 0.5 fusion.61
  26.4 0.9 fusion.21
  27.3 0.7 fusion.18
  28.1 0.4 convolution_bitcast_fusion
  28.5 0.8 copy-done
  29.3 0.9 fusion.3
  30.2 0.6 fusion.25
  30.9 0.7 collective-permute-start.4
  31.8 2.8 %collective-permute-start.3 = (bf16[128,2,256]{0,2,1:T(8,128)(2,1)S(1)}, bf16[128,2,256]{0,2,1:T(8,128)(2,1)S(1)}, u32[]{:S(2)}, u32[]{:S(2)}) collective-permute-start(bf16[128,2,256]{0,2,1:T(8,128)(2,1)S(1)} %get-tuple-element.14), channel_id=1, source_target_pairs={{64,0},{128,64},{192,128},{320,256},{384,320},{448,384},{576,512},... | collective-permute-start | bytes 393224 | tf_op jit(solution)/shard_map/ppermute | solution.py:21
  34.6 3.0 %collective-permute-start.5 = (bf16[128,2,256]{0,2,1:T(8,128)(2,1)S(1)}, bf16[128,2,256]{0,2,1:T(8,128)(2,1)S(1)}, u32[]{:S(2)}, u32[]{:S(2)}) collective-permute-start(bf16[128,2,256]{0,2,1:T(8,128)(2,1)S(1)} %fusion.34), channel_id=1, source_target_pairs={{128,0},{192,64},{256,128},{320,192},{384,256},{448,320},{512,384}... | collective-permute-start | bytes 393224 | tf_op jit(solution)/shard_map/ppermute | solution.py:21
  37.7 33.6 %collective-permute-done.5 = bf16[128,2,256]{0,2,1:T(8,128)(2,1)S(1)} collective-permute-done((bf16[128,2,256]{0,2,1:T(8,128)(2,1)S(1)}, bf16[128,2,256]{0,2,1:T(8,128)(2,1)S(1)}, u32[]{:S(2)}, u32[]{:S(2)}) %collective-permute-start.5) | collective-permute-done | bytes 131104 | tf_op jit(solution)/shard_map/ppermute | solution.py:21
  71.6 1.8 %multiply_bitcast_fusion = bf16[8,2,64,2,256]{4,1,3,2,0:T(2,128)(2,1)} fusion(bf16[2,8]{0,1:T(8,128)(2,1)S(1)} %fusion.46, bf16[2,64,2,256]{3,0,2,1:T(2,128)(2,1)S(1)} %copy.102), kind=kLoop, calls=%fused_computation.29 | loop fusion | flops 524288 | bytes 1179680 | tf_op jit(solution)/shard_map/cp,pxhw->cpxhw/transpose | solution.py:143
  73.4 20.7 %all-to-all-start = ((bf16[8,2,64,2,256]{4,1,3,2,0:T(2,128)(2,1)}), bf16[8,2,64,2,256]{4,1,3,2,0:T(2,128)(2,1)S(1)}, u32[]{:S(2)}, u32[]{:S(2)}) async-start(bf16[8,2,64,2,256]{4,1,3,2,0:T(2,128)(2,1)} %multiply_bitcast_fusion), calls=%async_computation | async-start | bytes 2097152 | tf_op jit(solution)/shard_map/all_to_all | solution.py:146
  94.4 0.6 gather_fusion
  95.4 49.0 %all-to-all-done = bf16[8,2,64,2,256]{4,1,3,2,0:T(2,128)(2,1)S(1)} async-done(((bf16[8,2,64,2,256]{4,1,3,2,0:T(2,128)(2,1)}), bf16[8,2,64,2,256]{4,1,3,2,0:T(2,128)(2,1)S(1)}, u32[]{:S(2)}, u32[]{:S(2)}) %all-to-all-start) | async-done | bytes 1048608 | tf_op jit(solution)/shard_map/all_to_all | solution.py:146
  144.4 2.0 %bitcast_convert_fusion = bf16[4,4,64,2,256]{4,1,3,2,0:T(4,128)(2,1)} fusion(bf16[8,2,64,2,256]{4,1,3,2,0:T(2,128)(2,1)S(1)} %all-to-all-done, pred[4,8,2]{1,0,2:T(4,128)(4,1)S(1)} %iota_compare_fusion.2, pred[4,8,2]{1,2,0:T(4,128)(4,1)S(1)} %broadcast_compare_fusion), kind=kOutput, calls=%fused_computation.7 | convolution fusion | flops 17301760 | bytes 2097280 | tf_op jit(solution)/shard_map/tkzp,zpxhw->tkxhw/dot_general | solution.py:162
  146.4 4.3 %all-to-all-start.1 = ((bf16[4,4,64,2,256]{4,1,3,2,0:T(4,128)(2,1)}), bf16[4,4,64,2,256]{4,1,3,2,0:T(4,128)(2,1)S(1)}, u32[]{:S(2)}, u32[]{:S(2)}) async-start(bf16[4,4,64,2,256]{4,1,3,2,0:T(4,128)(2,1)} %bitcast_convert_fusion), calls=%async_computation.1 | async-start | bytes 2097152 | tf_op jit(solution)/shard_map/all_to_all | solution.py:165
  150.7 0.5 fusion.17
  151.2 1.0 copy.105
  152.2 9.4 %all-to-all-done.1 = bf16[4,4,64,2,256]{4,1,3,2,0:T(4,128)(2,1)S(1)} async-done(((bf16[4,4,64,2,256]{4,1,3,2,0:T(4,128)(2,1)}), bf16[4,4,64,2,256]{4,1,3,2,0:T(4,128)(2,1)S(1)}, u32[]{:S(2)}, u32[]{:S(2)}) %all-to-all-start.1) | async-done | bytes 1048608 | tf_op jit(solution)/shard_map/all_to_all | solution.py:165
  161.6 0.7 reduce_sum.42
  162.4 1.0 copy.106
  (43 shorter events, 1.9 us)
Async XLA Ops:
  0.6 19.3 %copy-start.3 = (bf16[1,128,2048]{2,1,0:T(8,128)(2,1)S(1)}, bf16[1,128,2048]{2,1,0:T(8,128)(2,1)}, u32[]{:S(2)}) copy-start(bf16[1,128,2048]{2,1,0:T(8,128)(2,1)} %param.7) | copy-start | bytes 1572868
  1.6 20.6 %collective-permute-start = (bf16[128,2,256]{2,0,1:T(8,128)(2,1)S(1)}, bf16[128,2,256]{2,0,1:T(8,128)(2,1)S(1)}, u32[]{:S(2)}, u32[]{:S(2)}) collective-permute-start(bf16[128,2,256]{2,0,1:T(8,128)(2,1)S(1)} %bitcast.119), channel_id=1, source_target_pairs={{0,64},{64,128},{128,192},{192,256},{256,320},{320,384},{384,448},... | collective-permute-start | bytes 393224 | tf_op jit(solution)/shard_map/ppermute | solution.py:15
  17.0 8.4 %collective-permute-start.1 = (bf16[128,2,256]{2,0,1:T(8,128)(2,1)S(1)}, bf16[128,2,256]{2,0,1:T(8,128)(2,1)S(1)}, u32[]{:S(2)}, u32[]{:S(2)}) collective-permute-start(bf16[128,2,256]{2,0,1:T(8,128)(2,1)S(1)} %bitcast.120), channel_id=1, source_target_pairs={{0,128},{64,192},{128,256},{256,384},{320,448},{384,512},{512,640}... | collective-permute-start | bytes 393224 | tf_op jit(solution)/shard_map/ppermute | solution.py:21
  22.3 3.1 %collective-permute-start.2 = (bf16[128,2,256]{2,0,1:T(8,128)(2,1)S(1)}, bf16[128,2,256]{2,0,1:T(8,128)(2,1)S(1)}, u32[]{:S(2)}, u32[]{:S(2)}) collective-permute-start(bf16[128,2,256]{2,0,1:T(8,128)(2,1)S(1)} %collective-permute-done), channel_id=1, source_target_pairs={{256,320},{512,576},{768,832},{257,321},{513,577},{769,833},{258,3... | collective-permute-start | bytes 393224 | tf_op jit(solution)/shard_map/ppermute | solution.py:21
  27.3 0.8 copy-start.1
  28.1 1.2 copy-start
  30.2 1.4 copy-start.4
  30.9 3.7 %collective-permute-start.4 = (f32[128,2,256]{0,2,1:T(8,128)S(1)}, f32[128,2,256]{0,2,1:T(8,128)S(1)}, u32[]{:S(2)}, u32[]{:S(2)}) collective-permute-start(f32[128,2,256]{0,2,1:T(8,128)S(1)} %get-tuple-element.15), channel_id=1, source_target_pairs={{256,320},{512,576},{768,832},{257,321},{513,577},{769,833},{258,3... | collective-permute-start | bytes 786440 | tf_op jit(solution)/shard_map/ppermute | solution.py:21
  31.8 5.9 %collective-permute-start.3 = (bf16[128,2,256]{0,2,1:T(8,128)(2,1)S(1)}, bf16[128,2,256]{0,2,1:T(8,128)(2,1)S(1)}, u32[]{:S(2)}, u32[]{:S(2)}) collective-permute-start(bf16[128,2,256]{0,2,1:T(8,128)(2,1)S(1)} %get-tuple-element.14), channel_id=1, source_target_pairs={{64,0},{128,64},{192,128},{320,256},{384,320},{448,384},{576,512},... | collective-permute-start | bytes 393224 | tf_op jit(solution)/shard_map/ppermute | solution.py:21
  34.6 36.7 %collective-permute-start.5 = (bf16[128,2,256]{0,2,1:T(8,128)(2,1)S(1)}, bf16[128,2,256]{0,2,1:T(8,128)(2,1)S(1)}, u32[]{:S(2)}, u32[]{:S(2)}) collective-permute-start(bf16[128,2,256]{0,2,1:T(8,128)(2,1)S(1)} %fusion.34), channel_id=1, source_target_pairs={{128,0},{192,64},{256,128},{320,192},{384,256},{448,320},{512,384}... | collective-permute-start | bytes 393224 | tf_op jit(solution)/shard_map/ppermute | solution.py:21
  73.4 71.0 %all-to-all-start = ((bf16[8,2,64,2,256]{4,1,3,2,0:T(2,128)(2,1)}), bf16[8,2,64,2,256]{4,1,3,2,0:T(2,128)(2,1)S(1)}, u32[]{:S(2)}, u32[]{:S(2)}) async-start(bf16[8,2,64,2,256]{4,1,3,2,0:T(2,128)(2,1)} %multiply_bitcast_fusion), calls=%async_computation | async-start | bytes 2097152 | tf_op jit(solution)/shard_map/all_to_all | solution.py:146
  95.4 55.3 %copy-start.2 = (bf16[384,2,256]{2,0,1:T(8,128)(2,1)S(1)}, bf16[384,2,256]{2,0,1:T(8,128)(2,1)}, u32[]{:S(2)}) copy-start(bf16[384,2,256]{2,0,1:T(8,128)(2,1)} %copy-done.1) | copy-start | bytes 1179652
  146.4 15.2 %all-to-all-start.1 = ((bf16[4,4,64,2,256]{4,1,3,2,0:T(4,128)(2,1)}), bf16[4,4,64,2,256]{4,1,3,2,0:T(4,128)(2,1)S(1)}, u32[]{:S(2)}, u32[]{:S(2)}) async-start(bf16[4,4,64,2,256]{4,1,3,2,0:T(4,128)(2,1)} %bitcast_convert_fusion), calls=%async_computation.1 | async-start | bytes 2097152 | tf_op jit(solution)/shard_map/all_to_all | solution.py:165

commit v8 on v5

--- a/solution.py
+++ b/solution.py
@@ -139,10 +139,12 @@
         & (piece_rank[None, None, :, :] == slot_ids[None, :, None, None])
     ).astype(jnp.bfloat16)
     second_out = jnp.einsum(
-        "tkzp,zpxhw->tkxhw", second_map, first_in, preferred_element_type=jnp.float32
-    ).astype(jnp.bfloat16)
+        "tkzp,zpxhw->tkxhw", second_map, first_in, preferred_element_type=jnp.bfloat16
+    )
     second_in = lax.all_to_all(second_out, "sx", split_axis=0, concat_axis=0, tiled=True)
-    owned = jnp.sum(second_in.astype(jnp.float32), 0).astype(jnp.bfloat16)
+    owned = second_in[0]
+    for source in range(1, outer):
+        owned = owned + second_in[source]
     return (query_grad, owned.reshape(1, 2 * piece_count * PIECE, kv_heads, 2 * HD))
 
 

time: 166 us -> 165 us (level)
  no operation moved by 1% of the time
where the time goes in v8:
time: 165 us; the launch traced here: 163 us
  waiting for transfers between devices  88.7 us (54%)
  starting transfers between devices  54.8 us (33%)
  local copies, waits for them, and re-layouts  7.75 us (5%)
  matrix products  7.52 us (5%)
  other arithmetic  2.88 us (2%)
    all_to_all x1, waiting for transfers between devices, shards(): lax.all_to_all(first_out, 'sz', split_axis=0, concat_axis=0, tiled=True)  48.9 us
    ppermute x5, waiting for transfers between devices, moved(): return lax.ppermute(shard, axis, pairs)  29.7 us
    all_to_all x1, starting transfers between devices, shards(): lax.all_to_all(first_out, 'sz', split_axis=0, concat_axis=0, tiled=True)  27.1 us
    ppermute x1, starting transfers between devices, shifted(): return lax.ppermute(shard, axis, pairs)  15.4 us
    all_to_all x1, waiting for transfers between devices, shards(): lax.all_to_all(second_out, 'sx', split_axis=0, concat_axis=0, tiled=True)  9.39 us
    ppermute x5, starting transfers between devices, moved(): return lax.ppermute(shard, axis, pairs)  7.96 us
    all_to_all x1, starting transfers between devices, shards(): lax.all_to_all(second_out, 'sx', split_axis=0, concat_axis=0, tiled=True)  4.32 us
    unnamed x8, local copies, waits for them, and re-layouts  4.23 us
  transfers between devices with their start and end apart: 8, of which 5 were waited for; matrix products, arithmetic and copies ran while one was open for 4% of the time, Pallas kernels for 0%

profile of v8, /device:TPU:24, one launch (start us, length us, event | category | flops | bytes accessed | tf_op | source)
XLA Modules:
  0.0 162.5 jit_solution(11967407019717599917)
XLA Ops:
  0.6 0.9 copy.104
  1.6 15.4 %collective-permute-start = (bf16[128,2,256]{2,0,1:T(8,128)(2,1)S(1)}, bf16[128,2,256]{2,0,1:T(8,128)(2,1)S(1)}, u32[]{:S(2)}, u32[]{:S(2)}) collective-permute-start(bf16[128,2,256]{2,0,1:T(8,128)(2,1)S(1)} %bitcast.127), channel_id=1, source_target_pairs={{0,64},{64,128},{128,192},{192,256},{256,320},{320,384},{384,448},... | collective-permute-start | bytes 393224 | tf_op jit(solution)/shard_map/ppermute | solution.py:15
  16.9 1.3 collective-permute-start.1
  18.3 0.7 fusion.53
  19.1 0.7 collective-permute-done
  19.7 0.7 collective-permute-start.2
  20.4 0.2 and_and_fusion.2
  20.6 1.3 copy.98
  21.9 1.3 copy.64
  23.3 2.0 %collective-permute-done.1 = bf16[128,2,256]{2,0,1:T(8,128)(2,1)S(1)} collective-permute-done((bf16[128,2,256]{2,0,1:T(8,128)(2,1)S(1)}, bf16[128,2,256]{2,0,1:T(8,128)(2,1)S(1)}, u32[]{:S(2)}, u32[]{:S(2)}) %collective-permute-start.1) | collective-permute-done | bytes 131104 | tf_op jit(solution)/shard_map/ppermute | solution.py:21
  25.4 0.8 fusion.4
  26.2 0.9 fusion.16
  27.1 0.7 fusion.27
  27.8 2.1 %fusion.1 = bf16[2,8,128,384]{2,3,1,0:T(8,128)(2,1)S(1)} fusion(bf16[128,2,8,128]{0,3,2,1:T(8,128)(2,1)} %bitcast.125, f32[2,8,128]{2,1,0:T(8,128)S(1)} %bitcast.132, f32[2,8,128]{2,1,0:T(8,128)S(1)} %get-tuple-element.21, f32[2,384,128,8]{2,1,3,0:T(8,128)S(1)} %get-tuple-element.22, pred[128,384]{0,1:T(8,128)(4,1)S(1)} %pad_add_fusion, ...), kind=kOutput, calls=%fused_computation.3 | convolution fusion | flops 206045184 | bytes 5505024 | tf_op jit(solution)/shard_map/igad,jgd->gaij/dot_general | solution.py:76
  29.9 0.6 fusion.20
  30.5 0.7 collective-permute-start.4
  31.2 0.2 fusion.47
  31.4 2.3 %collective-permute-start.3 = (bf16[128,2,256]{0,2,1:T(8,128)(2,1)S(1)}, bf16[128,2,256]{0,2,1:T(8,128)(2,1)S(1)}, u32[]{:S(2)}, u32[]{:S(2)}) collective-permute-start(bf16[128,2,256]{0,2,1:T(8,128)(2,1)S(1)} %get-tuple-element.12), channel_id=1, source_target_pairs={{64,0},{128,64},{192,128},{320,256},{384,320},{448,384},{576,512},... | collective-permute-start | bytes 393224 | tf_op jit(solution)/shard_map/ppermute | solution.py:21
  33.8 3.0 %collective-permute-start.5 = (bf16[128,2,256]{0,2,1:T(8,128)(2,1)S(1)}, bf16[128,2,256]{0,2,1:T(8,128)(2,1)S(1)}, u32[]{:S(2)}, u32[]{:S(2)}) collective-permute-start(bf16[128,2,256]{0,2,1:T(8,128)(2,1)S(1)} %fusion.39), channel_id=1, source_target_pairs={{128,0},{192,64},{256,128},{320,192},{384,256},{448,320},{512,384}... | collective-permute-start | bytes 393224 | tf_op jit(solution)/shard_map/ppermute | solution.py:21
  36.8 27.7 %collective-permute-done.5 = bf16[128,2,256]{0,2,1:T(8,128)(2,1)S(1)} collective-permute-done((bf16[128,2,256]{0,2,1:T(8,128)(2,1)S(1)}, bf16[128,2,256]{0,2,1:T(8,128)(2,1)S(1)}, u32[]{:S(2)}, u32[]{:S(2)}) %collective-permute-start.5) | collective-permute-done | bytes 131104 | tf_op jit(solution)/shard_map/ppermute | solution.py:21
  64.7 0.1 copy.76
  64.8 1.8 %multiply_bitcast_fusion = bf16[8,2,64,2,256]{4,1,3,2,0:T(2,128)(2,1)} fusion(bf16[2,8]{0,1:T(8,128)(2,1)S(1)} %fusion.46, bf16[2,64,2,256]{3,0,2,1:T(2,128)(2,1)S(1)} %copy.76), kind=kLoop, calls=%fused_computation.27 | loop fusion | flops 524288 | bytes 1179680 | tf_op jit(solution)/shard_map/cp,pxhw->cpxhw/transpose | solution.py:122
  66.6 27.1 %all-to-all-start = ((bf16[8,2,64,2,256]{4,1,3,2,0:T(2,128)(2,1)}), bf16[8,2,64,2,256]{4,1,3,2,0:T(2,128)(2,1)S(1)}, u32[]{:S(2)}, u32[]{:S(2)}) async-start(bf16[8,2,64,2,256]{4,1,3,2,0:T(2,128)(2,1)} %multiply_bitcast_fusion), calls=%async_computation | async-start | bytes 2097152 | tf_op jit(solution)/shard_map/all_to_all | solution.py:125
  94.1 0.6 gather_fusion
  95.1 48.9 %all-to-all-done = bf16[8,2,64,2,256]{4,1,3,2,0:T(2,128)(2,1)S(1)} async-done(((bf16[8,2,64,2,256]{4,1,3,2,0:T(2,128)(2,1)}), bf16[8,2,64,2,256]{4,1,3,2,0:T(2,128)(2,1)S(1)}, u32[]{:S(2)}, u32[]{:S(2)}) %all-to-all-start) | async-done | bytes 1048608 | tf_op jit(solution)/shard_map/all_to_all | solution.py:125
  144.0 2.0 %convolution_bitcast_fusion = bf16[4,4,64,2,256]{4,1,3,2,0:T(4,128)(2,1)} fusion(bf16[8,2,64,2,256]{4,1,3,2,0:T(2,128)(2,1)S(1)} %all-to-all-done, pred[4,8,2]{1,0,2:T(4,128)(4,1)S(1)} %iota_compare_fusion.2, pred[4,8,2]{1,2,0:T(4,128)(4,1)S(1)} %broadcast_compare_fusion), kind=kOutput, calls=%fused_computation.14 | convolution fusion | flops 16777472 | bytes 2097280 | tf_op jit(solution)/shard_map/tkzp,zpxhw->tkxhw/dot_general | solution.py:141
  146.0 4.3 %all-to-all-start.1 = ((bf16[4,4,64,2,256]{4,1,3,2,0:T(4,128)(2,1)}), bf16[4,4,64,2,256]{4,1,3,2,0:T(4,128)(2,1)S(1)}, u32[]{:S(2)}, u32[]{:S(2)}) async-start(bf16[4,4,64,2,256]{4,1,3,2,0:T(4,128)(2,1)} %convolution_bitcast_fusion), calls=%async_computation.1 | async-start | bytes 2097152 | tf_op jit(solution)/shard_map/all_to_all | solution.py:144
  150.4 0.5 fusion.15
  150.9 1.0 copy.79
  151.9 9.4 %all-to-all-done.1 = bf16[4,4,64,2,256]{4,1,3,2,0:T(4,128)(2,1)S(1)} async-done(((bf16[4,4,64,2,256]{4,1,3,2,0:T(4,128)(2,1)}), bf16[4,4,64,2,256]{4,1,3,2,0:T(4,128)(2,1)S(1)}, u32[]{:S(2)}, u32[]{:S(2)}) %all-to-all-start.1) | async-done | bytes 1048608 | tf_op jit(solution)/shard_map/all_to_all | solution.py:144
  161.3 0.2 slice_add_fusion
  161.5 1.0 copy.80
  (33 shorter events, 1.1 us)
Async XLA Ops:
  1.6 18.2 %collective-permute-start = (bf16[128,2,256]{2,0,1:T(8,128)(2,1)S(1)}, bf16[128,2,256]{2,0,1:T(8,128)(2,1)S(1)}, u32[]{:S(2)}, u32[]{:S(2)}) collective-permute-start(bf16[128,2,256]{2,0,1:T(8,128)(2,1)S(1)} %bitcast.127), channel_id=1, source_target_pairs={{0,64},{64,128},{128,192},{192,256},{256,320},{320,384},{384,448},... | collective-permute-start | bytes 393224 | tf_op jit(solution)/shard_map/ppermute | solution.py:15
  16.9 8.4 %collective-permute-start.1 = (bf16[128,2,256]{2,0,1:T(8,128)(2,1)S(1)}, bf16[128,2,256]{2,0,1:T(8,128)(2,1)S(1)}, u32[]{:S(2)}, u32[]{:S(2)}) collective-permute-start(bf16[128,2,256]{2,0,1:T(8,128)(2,1)S(1)} %bitcast.128), channel_id=1, source_target_pairs={{0,128},{64,192},{128,256},{256,384},{320,448},{384,512},{512,640}... | collective-permute-start | bytes 393224 | tf_op jit(solution)/shard_map/ppermute | solution.py:21
  19.7 5.6 %collective-permute-start.2 = (bf16[128,2,256]{2,0,1:T(8,128)(2,1)S(1)}, bf16[128,2,256]{2,0,1:T(8,128)(2,1)S(1)}, u32[]{:S(2)}, u32[]{:S(2)}) collective-permute-start(bf16[128,2,256]{2,0,1:T(8,128)(2,1)S(1)} %collective-permute-done), channel_id=1, source_target_pairs={{256,320},{512,576},{768,832},{257,321},{513,577},{769,833},{258,3... | collective-permute-start | bytes 393224 | tf_op jit(solution)/shard_map/ppermute | solution.py:21
  23.3 3.8 %copy-start = (bf16[1,128,2048]{1,2,0:T(8,128)(2,1)}, bf16[1,128,2048]{1,2,0:T(8,128)(2,1)S(1)}, u32[]{:S(2)}) copy-start(bf16[1,128,2048]{1,2,0:T(8,128)(2,1)S(1)} %copy.64) | copy-start | bytes 1572868
  29.9 1.4 copy-start.1
  30.5 3.2 %collective-permute-start.4 = (f32[128,2,256]{0,2,1:T(8,128)S(1)}, f32[128,2,256]{0,2,1:T(8,128)S(1)}, u32[]{:S(2)}, u32[]{:S(2)}) collective-permute-start(f32[128,2,256]{0,2,1:T(8,128)S(1)} %get-tuple-element.13), channel_id=1, source_target_pairs={{256,320},{512,576},{768,832},{257,321},{513,577},{769,833},{258,3... | collective-permute-start | bytes 786440 | tf_op jit(solution)/shard_map/ppermute | solution.py:21
  31.4 5.4 %collective-permute-start.3 = (bf16[128,2,256]{0,2,1:T(8,128)(2,1)S(1)}, bf16[128,2,256]{0,2,1:T(8,128)(2,1)S(1)}, u32[]{:S(2)}, u32[]{:S(2)}) collective-permute-start(bf16[128,2,256]{0,2,1:T(8,128)(2,1)S(1)} %get-tuple-element.12), channel_id=1, source_target_pairs={{64,0},{128,64},{192,128},{320,256},{384,320},{448,384},{576,512},... | collective-permute-start | bytes 393224 | tf_op jit(solution)/shard_map/ppermute | solution.py:21
  33.8 30.7 %collective-permute-start.5 = (bf16[128,2,256]{0,2,1:T(8,128)(2,1)S(1)}, bf16[128,2,256]{0,2,1:T(8,128)(2,1)S(1)}, u32[]{:S(2)}, u32[]{:S(2)}) collective-permute-start(bf16[128,2,256]{0,2,1:T(8,128)(2,1)S(1)} %fusion.39), channel_id=1, source_target_pairs={{128,0},{192,64},{256,128},{320,192},{384,256},{448,320},{512,384}... | collective-permute-start | bytes 393224 | tf_op jit(solution)/shard_map/ppermute | solution.py:21
  66.6 77.4 %all-to-all-start = ((bf16[8,2,64,2,256]{4,1,3,2,0:T(2,128)(2,1)}), bf16[8,2,64,2,256]{4,1,3,2,0:T(2,128)(2,1)S(1)}, u32[]{:S(2)}, u32[]{:S(2)}) async-start(bf16[8,2,64,2,256]{4,1,3,2,0:T(2,128)(2,1)} %multiply_bitcast_fusion), calls=%async_computation | async-start | bytes 2097152 | tf_op jit(solution)/shard_map/all_to_all | solution.py:125
  146.0 15.2 %all-to-all-start.1 = ((bf16[4,4,64,2,256]{4,1,3,2,0:T(4,128)(2,1)}), bf16[4,4,64,2,256]{4,1,3,2,0:T(4,128)(2,1)S(1)}, u32[]{:S(2)}, u32[]{:S(2)}) async-start(bf16[4,4,64,2,256]{4,1,3,2,0:T(4,128)(2,1)} %convolution_bitcast_fusion), calls=%async_computation.1 | async-start | bytes 2097152 | tf_op jit(solution)/shard_map/all_to_all | solution.py:144

commit v9 on v8

--- a/solution.py
+++ b/solution.py
@@ -116,12 +116,7 @@
     route_table = route[0]
     seq_count = route_table.shape[0]
     piece_rows = kv_grad.reshape(piece_count, PIECE, kv_heads, 2 * HD)
-    my_route = lax.dynamic_index_in_dim(route_table, row_index * inner + col_index, 0, keepdims=False)
-    col_ids = jnp.arange(inner, dtype=jnp.int32)
-    to_col = (my_route[None, :] % inner == col_ids[:, None]).astype(jnp.bfloat16)
-    first_out = jnp.einsum(
-        "cp,pxhw->cpxhw", to_col, piece_rows, preferred_element_type=jnp.bfloat16
-    )
+    first_out = jnp.broadcast_to(piece_rows[None], (inner,) + piece_rows.shape)
     first_in = lax.all_to_all(first_out, "sz", split_axis=0, concat_axis=0, tiled=True)
     row_routes = lax.dynamic_slice_in_dim(route_table, row_index * inner, inner, 0)
     owners = jnp.arange(seq_count, dtype=jnp.int32)

time: 165 us -> 164 us (level)
  other arithmetic: 2.88 us -> 1.05 us
    transpose x1 -> x0, other arithmetic: 1.82 us -> none  [shards(): jnp.einsum('cp,pxhw->cpxhw', to_col, piece_rows, preferred_element_type=j...]
    broadcast_in_dim x0 -> x2, local copies, waits for them, and re-layouts: none -> 1.65 us  [shards(): first_out = jnp.broadcast_to(piece_rows[None], (inner,) + piece_rows.shape)]
    unnamed x8 -> x6, local copies, waits for them, and re-layouts: 4.23 us -> 4.22 us
where the time goes in v9:
time: 164 us; the launch traced here: 161 us
  waiting for transfers between devices  88.9 us (54%)
  starting transfers between devices  54.8 us (33%)
  local copies, waits for them, and re-layouts  9.07 us (6%)
  matrix products  6.48 us (4%)
    all_to_all x1, waiting for transfers between devices, shards(): lax.all_to_all(first_out, 'sz', split_axis=0, concat_axis=0, tiled=True)  48.9 us
    ppermute x5, waiting for transfers between devices, moved(): return lax.ppermute(shard, axis, pairs)  29.9 us
    all_to_all x1, starting transfers between devices, shards(): lax.all_to_all(first_out, 'sz', split_axis=0, concat_axis=0, tiled=True)  27.1 us
    ppermute x1, starting transfers between devices, shifted(): return lax.ppermute(shard, axis, pairs)  15.4 us
    all_to_all x1, waiting for transfers between devices, shards(): lax.all_to_all(second_out, 'sx', split_axis=0, concat_axis=0, tiled=True)  9.39 us
    ppermute x5, starting transfers between devices, moved(): return lax.ppermute(shard, axis, pairs)  7.96 us
    all_to_all x1, starting transfers between devices, shards(): lax.all_to_all(second_out, 'sx', split_axis=0, concat_axis=0, tiled=True)  4.33 us
    unnamed x6, local copies, waits for them, and re-layouts  4.22 us
  transfers between devices with their start and end apart: 8, of which 5 were waited for; matrix products, arithmetic and copies ran while one was open for 4% of the time, Pallas kernels for 0%

profile of v9, /device:TPU:24, one launch (start us, length us, event | category | flops | bytes accessed | tf_op | source)
XLA Modules:
  0.0 161.2 jit_solution(12043565006437421728)
XLA Ops:
  0.6 0.9 copy.104
  1.6 15.4 %collective-permute-start = (bf16[128,2,256]{2,0,1:T(8,128)(2,1)S(1)}, bf16[128,2,256]{2,0,1:T(8,128)(2,1)S(1)}, u32[]{:S(2)}, u32[]{:S(2)}) collective-permute-start(bf16[128,2,256]{2,0,1:T(8,128)(2,1)S(1)} %bitcast.123), channel_id=1, source_target_pairs={{0,64},{64,128},{128,192},{192,256},{256,320},{320,384},{384,448},... | collective-permute-start | bytes 393224 | tf_op jit(solution)/shard_map/ppermute | solution.py:15
  16.9 1.3 collective-permute-start.1
  18.3 0.7 fusion.50
  19.1 0.7 collective-permute-done
  19.7 0.7 collective-permute-start.2
  20.4 0.2 and_and_fusion.2
  20.6 1.3 copy.98
  21.9 1.3 copy.64
  23.3 2.0 %collective-permute-done.1 = bf16[128,2,256]{2,0,1:T(8,128)(2,1)S(1)} collective-permute-done((bf16[128,2,256]{2,0,1:T(8,128)(2,1)S(1)}, bf16[128,2,256]{2,0,1:T(8,128)(2,1)S(1)}, u32[]{:S(2)}, u32[]{:S(2)}) %collective-permute-start.1) | collective-permute-done | bytes 131104 | tf_op jit(solution)/shard_map/ppermute | solution.py:21
  25.4 0.8 fusion.4
  26.2 0.9 fusion.16
  27.0 0.7 fusion.27
  27.8 1.0 fusion.1
  28.8 0.6 fusion.20
  29.5 0.7 collective-permute-start.4
  30.1 2.3 %collective-permute-start.3 = (bf16[128,2,256]{0,2,1:T(8,128)(2,1)S(1)}, bf16[128,2,256]{0,2,1:T(8,128)(2,1)S(1)}, u32[]{:S(2)}, u32[]{:S(2)}) collective-permute-start(bf16[128,2,256]{0,2,1:T(8,128)(2,1)S(1)} %get-tuple-element.12), channel_id=1, source_target_pairs={{64,0},{128,64},{192,128},{320,256},{384,320},{448,384},{576,512},... | collective-permute-start | bytes 393224 | tf_op jit(solution)/shard_map/ppermute | solution.py:21
  32.5 3.0 %collective-permute-start.5 = (bf16[128,2,256]{0,2,1:T(8,128)(2,1)S(1)}, bf16[128,2,256]{0,2,1:T(8,128)(2,1)S(1)}, u32[]{:S(2)}, u32[]{:S(2)}) collective-permute-start(bf16[128,2,256]{0,2,1:T(8,128)(2,1)S(1)} %fusion.39), channel_id=1, source_target_pairs={{128,0},{192,64},{256,128},{320,192},{384,256},{448,320},{512,384}... | collective-permute-start | bytes 393224 | tf_op jit(solution)/shard_map/ppermute | solution.py:21
  35.6 27.9 %collective-permute-done.5 = bf16[128,2,256]{0,2,1:T(8,128)(2,1)S(1)} collective-permute-done((bf16[128,2,256]{0,2,1:T(8,128)(2,1)S(1)}, bf16[128,2,256]{0,2,1:T(8,128)(2,1)S(1)}, u32[]{:S(2)}, u32[]{:S(2)}) %collective-permute-start.5) | collective-permute-done | bytes 131104 | tf_op jit(solution)/shard_map/ppermute | solution.py:21
  63.5 0.1 copy.75
  63.6 0.1 copy.76
  63.8 1.5 broadcast_in_dim.15
  65.3 27.1 %all-to-all-start = ((bf16[8,2,64,2,256]{4,1,3,2,0:T(2,128)(2,1)}), bf16[8,2,64,2,256]{4,1,3,2,0:T(2,128)(2,1)S(1)}, u32[]{:S(2)}, u32[]{:S(2)}) async-start(bf16[8,2,64,2,256]{4,1,3,2,0:T(2,128)(2,1)} %broadcast_in_dim.15), calls=%async_computation | async-start | bytes 2097152 | tf_op jit(solution)/shard_map/all_to_all | solution.py:120
  92.8 0.6 gather_fusion
  93.7 48.9 %all-to-all-done = bf16[8,2,64,2,256]{4,1,3,2,0:T(2,128)(2,1)S(1)} async-done(((bf16[8,2,64,2,256]{4,1,3,2,0:T(2,128)(2,1)}), bf16[8,2,64,2,256]{4,1,3,2,0:T(2,128)(2,1)S(1)}, u32[]{:S(2)}, u32[]{:S(2)}) %all-to-all-start) | async-done | bytes 1048608 | tf_op jit(solution)/shard_map/all_to_all | solution.py:120
  142.7 2.0 %convolution_bitcast_fusion = bf16[4,4,64,2,256]{4,1,3,2,0:T(4,128)(2,1)} fusion(bf16[8,2,64,2,256]{4,1,3,2,0:T(2,128)(2,1)S(1)} %all-to-all-done, pred[4,8,2]{1,0,2:T(4,128)(4,1)S(1)} %iota_compare_fusion.1, pred[4,8,2]{1,2,0:T(4,128)(4,1)S(1)} %broadcast_compare_fusion), kind=kOutput, calls=%fused_computation.14 | convolution fusion | flops 16777472 | bytes 2097280 | tf_op jit(solution)/shard_map/tkzp,zpxhw->tkxhw/dot_general | solution.py:136
  144.7 4.3 %all-to-all-start.1 = ((bf16[4,4,64,2,256]{4,1,3,2,0:T(4,128)(2,1)}), bf16[4,4,64,2,256]{4,1,3,2,0:T(4,128)(2,1)S(1)}, u32[]{:S(2)}, u32[]{:S(2)}) async-start(bf16[4,4,64,2,256]{4,1,3,2,0:T(4,128)(2,1)} %convolution_bitcast_fusion), calls=%async_computation.1 | async-start | bytes 2097152 | tf_op jit(solution)/shard_map/all_to_all | solution.py:139
  149.0 0.5 fusion.15
  149.5 1.0 copy.79
  150.5 9.4 %all-to-all-done.1 = bf16[4,4,64,2,256]{4,1,3,2,0:T(4,128)(2,1)S(1)} async-done(((bf16[4,4,64,2,256]{4,1,3,2,0:T(4,128)(2,1)}), bf16[4,4,64,2,256]{4,1,3,2,0:T(4,128)(2,1)S(1)}, u32[]{:S(2)}, u32[]{:S(2)}) %all-to-all-start.1) | async-done | bytes 1048608 | tf_op jit(solution)/shard_map/all_to_all | solution.py:139
  159.9 0.2 slice_add_fusion
  160.2 1.0 copy.80
  (28 shorter events, 1.0 us)
Async XLA Ops:
  1.6 18.2 %collective-permute-start = (bf16[128,2,256]{2,0,1:T(8,128)(2,1)S(1)}, bf16[128,2,256]{2,0,1:T(8,128)(2,1)S(1)}, u32[]{:S(2)}, u32[]{:S(2)}) collective-permute-start(bf16[128,2,256]{2,0,1:T(8,128)(2,1)S(1)} %bitcast.123), channel_id=1, source_target_pairs={{0,64},{64,128},{128,192},{192,256},{256,320},{320,384},{384,448},... | collective-permute-start | bytes 393224 | tf_op jit(solution)/shard_map/ppermute | solution.py:15
  16.9 8.4 %collective-permute-start.1 = (bf16[128,2,256]{2,0,1:T(8,128)(2,1)S(1)}, bf16[128,2,256]{2,0,1:T(8,128)(2,1)S(1)}, u32[]{:S(2)}, u32[]{:S(2)}) collective-permute-start(bf16[128,2,256]{2,0,1:T(8,128)(2,1)S(1)} %bitcast.124), channel_id=1, source_target_pairs={{0,128},{64,192},{128,256},{256,384},{320,448},{384,512},{512,640}... | collective-permute-start | bytes 393224 | tf_op jit(solution)/shard_map/ppermute | solution.py:21
  19.7 5.6 %collective-permute-start.2 = (bf16[128,2,256]{2,0,1:T(8,128)(2,1)S(1)}, bf16[128,2,256]{2,0,1:T(8,128)(2,1)S(1)}, u32[]{:S(2)}, u32[]{:S(2)}) collective-permute-start(bf16[128,2,256]{2,0,1:T(8,128)(2,1)S(1)} %collective-permute-done), channel_id=1, source_target_pairs={{256,320},{512,576},{768,832},{257,321},{513,577},{769,833},{258,3... | collective-permute-start | bytes 393224 | tf_op jit(solution)/shard_map/ppermute | solution.py:21
  29.5 62.9 %copy-start = (s32[1,32,2]{1,2,0:T(2,128)S(1)}, s32[1,32,2]{1,2,0:T(2,128)}, u32[]{:S(2)}) copy-start(s32[1,32,2]{1,2,0:T(2,128)} %param.9) | copy-start | bytes 772
  29.5 3.0 %collective-permute-start.4 = (f32[128,2,256]{0,2,1:T(8,128)S(1)}, f32[128,2,256]{0,2,1:T(8,128)S(1)}, u32[]{:S(2)}, u32[]{:S(2)}) collective-permute-start(f32[128,2,256]{0,2,1:T(8,128)S(1)} %get-tuple-element.13), channel_id=1, source_target_pairs={{256,320},{512,576},{768,832},{257,321},{513,577},{769,833},{258,3... | collective-permute-start | bytes 786440 | tf_op jit(solution)/shard_map/ppermute | solution.py:21
  30.1 5.4 %collective-permute-start.3 = (bf16[128,2,256]{0,2,1:T(8,128)(2,1)S(1)}, bf16[128,2,256]{0,2,1:T(8,128)(2,1)S(1)}, u32[]{:S(2)}, u32[]{:S(2)}) collective-permute-start(bf16[128,2,256]{0,2,1:T(8,128)(2,1)S(1)} %get-tuple-element.12), channel_id=1, source_target_pairs={{64,0},{128,64},{192,128},{320,256},{384,320},{448,384},{576,512},... | collective-permute-start | bytes 393224 | tf_op jit(solution)/shard_map/ppermute | solution.py:21
  32.5 30.9 %collective-permute-start.5 = (bf16[128,2,256]{0,2,1:T(8,128)(2,1)S(1)}, bf16[128,2,256]{0,2,1:T(8,128)(2,1)S(1)}, u32[]{:S(2)}, u32[]{:S(2)}) collective-permute-start(bf16[128,2,256]{0,2,1:T(8,128)(2,1)S(1)} %fusion.39), channel_id=1, source_target_pairs={{128,0},{192,64},{256,128},{320,192},{384,256},{448,320},{512,384}... | collective-permute-start | bytes 393224 | tf_op jit(solution)/shard_map/ppermute | solution.py:21
  65.3 77.4 %all-to-all-start = ((bf16[8,2,64,2,256]{4,1,3,2,0:T(2,128)(2,1)}), bf16[8,2,64,2,256]{4,1,3,2,0:T(2,128)(2,1)S(1)}, u32[]{:S(2)}, u32[]{:S(2)}) async-start(bf16[8,2,64,2,256]{4,1,3,2,0:T(2,128)(2,1)} %broadcast_in_dim.15), calls=%async_computation | async-start | bytes 2097152 | tf_op jit(solution)/shard_map/all_to_all | solution.py:120
  144.7 15.2 %all-to-all-start.1 = ((bf16[4,4,64,2,256]{4,1,3,2,0:T(4,128)(2,1)}), bf16[4,4,64,2,256]{4,1,3,2,0:T(4,128)(2,1)S(1)}, u32[]{:S(2)}, u32[]{:S(2)}) async-start(bf16[4,4,64,2,256]{4,1,3,2,0:T(4,128)(2,1)} %convolution_bitcast_fusion), calls=%async_computation.1 | async-start | bytes 2097152 | tf_op jit(solution)/shard_map/all_to_all | solution.py:139
